TPU v7x, 128 devices: a whole 4x4x4 slice. The times are simulated.
128 devices in a mesh: expert: 16 (over z, x), dp: 8 (over y, core).
Axes of the slice: x: 4, y: 4, z: 4, core: 2. Of those that a mesh axis runs over, the one named last changes fastest.
Arguments:
- tokens: bfloat16 [16, 480, 7168], P('expert', 'dp'), may hold values from -6 to 6
- cotangent: bfloat16 [16, 480, 7168], P('expert', 'dp'), may hold values from -1.5 to 1.5
- counts: int32 [16, 8], replicated, may hold values from 1 to 60, as said below
- w_gate: bfloat16 [16, 7168, 2048], P('expert', None, 'dp'), may hold values from -0.0625 to 0.0625
- w_up: bfloat16 [16, 7168, 2048], P('expert', None, 'dp'), may hold values from -0.0625 to 0.0625
- w_down: bfloat16 [16, 2048, 7168], P('expert', 'dp'), may hold values from -0.125 to 0.125
Outputs:
- outputs: bfloat16 [16, 480, 7168], P('expert', 'dp')
- input_grads: bfloat16 [16, 480, 7168], P('expert', 'dp')
- gate_grad: bfloat16 [16, 7168, 2048], P('expert', None, 'dp')
- up_grad: bfloat16 [16, 7168, 2048], P('expert', None, 'dp')
- down_grad: bfloat16 [16, 2048, 7168], P('expert', 'dp')
Inputs may be any that keep to these rules, and one draw needn't show every extreme that they name: For each expert e below 8, exactly one of experts e and e + 8 is hot: all its counts exceed 40 - 20 and one equals 60; every count of the other is at most 20 and one equals 20.
All inputs are finite; a program needn't handle non-finite values.
Results may differ from a plain program's by a relative error of at most 0.012.
Values may be sent and summed in bfloat16 or wider, within the bound.
No kernel may reach another device: no remote copies, remote signals or barrier semaphores. Data moves between devices by JAX's collectives and lax.ppermute only.
A program may use at most 192 MiB of HBM per device.

v0:
```python
import jax
import jax.numpy as jnp
from jax import lax
from jax.sharding import PartitionSpec as P

HOME = 40
SPILL = 20


def swapped(x, axis, distance):
    return lax.ppermute(x, axis, [(i, i ^ 1 << distance) for i in range(lax.axis_size(axis))])


def silu_slope(value):
    sigma = jax.nn.sigmoid(value)
    return sigma * (1.0 + value * (1.0 - sigma))


def contract_last(left, right):
    return lax.dot_general(
        left, right, (((1,), (1,)), ((), ())), preferred_element_type=jnp.float32
    )


def contract_first(left, right):
    return lax.dot_general(
        left, right, (((0,), (0,)), ((), ())), preferred_element_type=jnp.float32
    )


def expert_work(rows, cot_rows, gate_w, up_w, down_w):
    gate = jnp.dot(rows, gate_w, preferred_element_type=jnp.float32)
    up = jnp.dot(rows, up_w, preferred_element_type=jnp.float32)
    active = jax.nn.silu(gate)
    hidden = (active * up).astype(jnp.bfloat16)
    out_part = jnp.dot(hidden, down_w, preferred_element_type=jnp.float32)
    hidden_grad = contract_last(cot_rows, down_w)
    gate_act = (hidden_grad * up * silu_slope(gate)).astype(jnp.bfloat16)
    up_act = (hidden_grad * active).astype(jnp.bfloat16)
    in_part = contract_last(gate_act, gate_w) + contract_last(up_act, up_w)
    gate_term = contract_first(rows, gate_act)
    up_term = contract_first(rows, up_act)
    down_term = contract_first(hidden, cot_rows)
    return (out_part, in_part, gate_term, up_term, down_term)


def shards(tokens, cotangent, counts, w_gate, w_up, w_down):
    rows_in = tokens[0]
    cot_in = cotangent[0]
    gate_w = w_gate[0]
    up_w = w_up[0]
    down_w = w_down[0]
    expert_total = lax.axis_size("expert")
    expert_pos = lax.axis_index("expert")
    batch_pos = lax.axis_index("dp")
    expert_ids = jnp.arange(counts.shape[0], dtype=jnp.int32)
    batch_ids = jnp.arange(counts.shape[1], dtype=jnp.int32)
    own_counts = jnp.sum(jnp.where(expert_ids[:, None] == expert_pos, counts, 0), axis=0)
    own_total = jnp.sum(jnp.where(batch_ids == batch_pos, own_counts, 0))
    own_hot = jnp.max(own_counts) > HOME - SPILL
    slots = rows_in.shape[0]
    valid = (jnp.arange(slots, dtype=jnp.int32) < own_total)[:, None]
    masked = jnp.where(valid, rows_in, jnp.zeros_like(rows_in))
    masked_cot = jnp.where(valid, cot_in, jnp.zeros_like(cot_in))
    partner_bit = expert_total.bit_length() - 2
    border = HOME - SPILL
    got_rows, got_cot, far_gate, far_up, far_down = swapped(
        (masked[HOME:], masked_cot[HOME:], gate_w, up_w, down_w), "expert", partner_bit
    )
    region_rows = masked[border:HOME] + got_rows
    region_cot = masked_cot[border:HOME] + got_cot
    pick_gate = jnp.where(own_hot, gate_w, far_gate)
    pick_up = jnp.where(own_hot, up_w, far_up)
    pick_down = jnp.where(own_hot, down_w, far_down)
    all_home, all_region, cot_home, cot_region = (
        lax.all_gather(masked[:border], "dp", axis=0, tiled=True),
        lax.all_gather(region_rows, "dp", axis=0, tiled=True),
        lax.all_gather(masked_cot[:border], "dp", axis=0, tiled=True),
        lax.all_gather(region_cot, "dp", axis=0, tiled=True),
    )
    home_res = expert_work(all_home, cot_home, gate_w, up_w, down_w)
    region_res = expert_work(all_region, cot_region, pick_gate, pick_up, pick_down)
    home_out, region_sum_out, home_in, region_sum_in = (
        lax.psum_scatter(
            home_res[0].astype(jnp.bfloat16), "dp", scatter_dimension=0, tiled=True
        ).astype(jnp.float32),
        lax.psum_scatter(
            region_res[0].astype(jnp.bfloat16), "dp", scatter_dimension=0, tiled=True
        ).astype(jnp.float32),
        lax.psum_scatter(
            home_res[1].astype(jnp.bfloat16), "dp", scatter_dimension=0, tiled=True
        ).astype(jnp.float32),
        lax.psum_scatter(
            region_res[1].astype(jnp.bfloat16), "dp", scatter_dimension=0, tiled=True
        ).astype(jnp.float32),
    )
    region_out = region_sum_out.astype(jnp.bfloat16)
    region_in = region_sum_in.astype(jnp.bfloat16)
    blank = jnp.zeros_like(region_out)
    back_out, back_in = swapped(
        (jnp.where(own_hot, blank, region_out), jnp.where(own_hot, blank, region_in)),
        "expert",
        partner_bit,
    )
    outputs = jnp.concatenate(
        [home_out.astype(jnp.bfloat16), jnp.where(own_hot, region_out, blank), back_out], axis=0
    )
    input_grads = jnp.concatenate(
        [home_in.astype(jnp.bfloat16), jnp.where(own_hot, region_in, blank), back_in], axis=0
    )
    kept = [home_res[k] + jnp.where(own_hot, region_res[k], 0.0) for k in (2, 3, 4)]
    sending = [jnp.where(own_hot, 0.0, region_res[k]).astype(jnp.bfloat16) for k in (2, 3, 4)]
    got_gate, got_up, got_down = swapped(
        (sending[0], sending[1], sending[2]), "expert", partner_bit
    )
    gate_grad = (kept[0] + got_gate.astype(jnp.float32)).astype(jnp.bfloat16)
    up_grad = (kept[1] + got_up.astype(jnp.float32)).astype(jnp.bfloat16)
    down_grad = (kept[2] + got_down.astype(jnp.float32)).astype(jnp.bfloat16)
    return (outputs[None], input_grads[None], gate_grad[None], up_grad[None], down_grad[None])


def solution(mesh):
    placed = (
        P("expert", "dp", None),
        P("expert", "dp", None),
        P(),
        P("expert", None, "dp"),
        P("expert", None, "dp"),
        P("expert", "dp", None),
    )
    return jax.shard_map(
        shards,
        mesh=mesh,
        in_specs=placed,
        out_specs=(
            P("expert", "dp", None),
            P("expert", "dp", None),
            P("expert", None, "dp"),
            P("expert", None, "dp"),
            P("expert", "dp", None),
        ),
        check_vma=False,
    )
```

profile of v0, /device:TPU:1, one launch (start us, length us, event | category | flops | bytes accessed | tf_op | source)
XLA Modules:
  0.0 691.9 jit_solution(14175474029074275268)
XLA Ops:
  7.2 0.8 select_reduce_fusion
  9.3 1.6 bitcast_select_fusion
  11.0 0.8 slice_bitcast_fusion
  12.7 4.5 collective-permute-start.5
  17.2 7.8 %collective-permute-done.5 = bf16[20,7168]{1,0:T(8,128)(2,1)S(1)} collective-permute-done((bf16[20,7168]{1,0:T(8,128)(2,1)S(1)}, bf16[20,7168]{1,0:T(8,128)(2,1)S(1)}, u32[]{:S(2)}, u32[]{:S(2)}) %collective-permute-start.5) | collective-permute-done | bytes 286752 | tf_op jit(solution)/shard_map/ppermute | solution.py:11
  25.0 0.8 fusion.13
  25.9 2.8 collective-permute-start
  28.6 7.2 %collective-permute-done = bf16[20,7168]{1,0:T(8,128)(2,1)S(1)} collective-permute-done((bf16[20,7168]{1,0:T(8,128)(2,1)S(1)}, bf16[20,7168]{1,0:T(8,128)(2,1)S(1)}, u32[]{:S(2)}, u32[]{:S(2)}) %collective-permute-start) | collective-permute-done | bytes 286752 | tf_op jit(solution)/shard_map/ppermute | solution.py:11
  35.8 0.8 fusion.14
  36.7 2.6 collective-permute-start.3
  39.8 2.5 collective-permute-start.1
  44.2 4.1 reshape.24
  48.4 22.2 %all-gather.9.cloned.1.call-done = bf16[8,20,7168]{2,1,0:T(8,128)(2,1)} async-done(((bf16[1,20,7168]{2,1,0:T(8,128)(2,1)}), bf16[8,20,7168]{2,1,0:T(8,128)(2,1)}) %all-gather.9.cloned.1.call-update) | async-done | bytes 2293776 | tf_op jit(solution)/shard_map/all_gather | solution.py:76
  70.6 2.7 reshape.20
  73.3 3.0 fusion.26
  76.5 0.8 fusion.32
  77.3 1.2 copy-done.6
  79.2 1.4 multiply_convert_fusion.2
  80.6 2.2 convolution_convert_fusion.1
  82.8 1.4 fusion.29
  84.2 0.9 copy-done.4
  85.1 2.8 fusion.4
  87.9 11.7 %all-gather.15.cloned.1.call-done = bf16[8,20,7168]{2,1,0:T(8,128)(2,1)} async-done(((bf16[1,20,7168]{2,1,0:T(8,128)(2,1)}), bf16[8,20,7168]{2,1,0:T(8,128)(2,1)}) %all-gather.15.cloned.1.call-update) | async-done | bytes 2293776 | tf_op jit(solution)/shard_map/all_gather | solution.py:79
  99.5 4.1 reshape.26
  103.7 24.7 %all-gather.11.cloned.1.call-done = bf16[8,20,7168]{2,1,0:T(8,128)(2,1)} async-done(((bf16[1,20,7168]{2,1,0:T(8,128)(2,1)}), bf16[8,20,7168]{2,1,0:T(8,128)(2,1)}) %all-gather.11.cloned.1.call-update) | async-done | bytes 2293776 | tf_op jit(solution)/shard_map/all_gather | solution.py:77
  128.3 4.1 reshape.22
  132.5 5.2 fusion.12
  137.6 58.4 %collective-permute-done.2 = bf16[7168,256]{1,0:T(8,128)(2,1)} collective-permute-done((bf16[7168,256]{1,0:T(8,128)(2,1)}, bf16[7168,256]{1,0:T(8,128)(2,1)}, u32[]{:S(2)}, u32[]{:S(2)}) %collective-permute-start.2) | collective-permute-done | bytes 3670048 | tf_op jit(solution)/shard_map/ppermute | solution.py:11
  196.0 3.0 fusion.11
  199.1 75.6 %collective-permute-done.1 = bf16[7168,256]{1,0:T(8,128)(2,1)} collective-permute-done((bf16[7168,256]{1,0:T(8,128)(2,1)}, bf16[7168,256]{1,0:T(8,128)(2,1)}, u32[]{:S(2)}, u32[]{:S(2)}) %collective-permute-start.1) | collective-permute-done | bytes 3670048 | tf_op jit(solution)/shard_map/ppermute | solution.py:11
  274.7 3.1 multiply_convert_fusion.1
  277.8 4.6 convolution_convert_fusion
  282.5 3.4 fusion.10
  285.9 5.1 fusion.5
  291.0 67.5 %fusion.34 = (bf16[24,7168]{1,0:T(8,128)(2,1)S(1)}, bf16[24,7168]{1,0:T(8,128)(2,1)}, bf16[24,7168]{1,0:T(8,128)(2,1)}, bf16[24,7168]{1,0:T(8,128)(2,1)S(1)}) fusion(bf16[160,7168]{1,0:T(8,128)(2,1)} %convolution_convert_fusion, bf16[160,7168]{1,0:T(8,128)(2,1)} %convolution_convert_fusion.1, bf16[160,7168]{1,0:T(8,128)(2,1)} %fusion.5, ...), kind=kCustom, calls=%all-reduce-scatter.4 | all-reduce-scatter fusion | flops 5505025 | bytes 10551808
  358.6 4.4 collective-permute-start.12
  363.0 1.6 slice.30
  364.5 2.3 collective-permute-start.10
  366.8 7.1 %select_convert_fusion = (bf16[256,7168]{1,0:T(8,128)(2,1)}, f32[256,7168]{1,0:T(8,128)}) fusion(pred[]{:T(512)S(6)} %gt.3, bf16[160,256]{1,0:T(8,128)(2,1)} %copy-done.12, bf16[160,7168]{1,0:T(8,128)(2,1)} %reshape.26), kind=kOutput, calls=%fused_computation.10 | convolution fusion | flops 589037568 | bytes 13385729 | tf_op jit(solution)/shard_map/dot_general | solution.py:26
  373.9 5.5 select_convert_fusion.2
  379.4 2.9 collective-permute-start.13
  382.3 5.3 select_convert_fusion.1
  387.6 4.0 collective-permute-start.16
  391.6 1.6 slice.33
  393.1 1.9 collective-permute-start.14
  395.7 2.2 collective-permute-start.15
  398.7 1.9 collective-permute-start.17
  400.7 7.9 %concatenate.9 = bf16[52,7168]{1,0:T(8,128)(2,1)S(1)} concatenate(bf16[4,7168]{1,0:T(4,128)(2,1)} %copy-done.19, bf16[24,7168]{1,0:T(8,128)(2,1)} %copy-done.11, bf16[24,7168]{1,0:T(8,128)(2,1)} %copy-done.10), dimensions={0} | concatenate | bytes 1490944
  408.5 1.0 broadcast_select_fusion.12
  409.5 1.9 collective-permute-start.11
  411.5 7.9 %concatenate.11 = bf16[52,7168]{1,0:T(8,128)(2,1)S(1)} concatenate(bf16[4,7168]{1,0:T(4,128)(2,1)} %collective-permute-done.17, bf16[24,7168]{1,0:T(8,128)(2,1)} %collective-permute-done.16, bf16[24,7168]{1,0:T(8,128)(2,1)} %get-tuple-element.13), dimensions={0} | concatenate | bytes 1490944
  419.3 1.0 broadcast_select_fusion.10
  420.4 3.0 collective-permute-start.7
  423.4 7.9 %concatenate.8 = bf16[52,7168]{1,0:T(8,128)(2,1)S(1)} concatenate(bf16[4,7168]{1,0:T(4,128)(2,1)} %collective-permute-done.11, bf16[24,7168]{1,0:T(8,128)(2,1)} %collective-permute-done.10, bf16[24,7168]{1,0:T(8,128)(2,1)} %get-tuple-element.12), dimensions={0} | concatenate | bytes 1490944
  431.3 3.0 collective-permute-start.4
  434.6 9.5 %concatenate.10 = bf16[52,7168]{1,0:T(8,128)(2,1)} concatenate(bf16[4,7168]{1,0:T(4,128)(2,1)} %collective-permute-done.15, bf16[24,7168]{1,0:T(8,128)(2,1)} %collective-permute-done.14, bf16[24,7168]{1,0:T(8,128)(2,1)S(1)} %get-tuple-element.14), dimensions={0} | concatenate | bytes 1490944
  444.2 1.3 constant_dynamic-slice_fusion
  445.5 212.5 %collective-permute-done.4 = bf16[20,7168]{1,0:T(8,128)(2,1)} collective-permute-done((bf16[20,7168]{1,0:T(8,128)(2,1)}, bf16[20,7168]{1,0:T(8,128)(2,1)}, u32[]{:S(2)}, u32[]{:S(2)}) %collective-permute-start.4) | collective-permute-done | bytes 286752 | tf_op jit(solution)/shard_map/ppermute | solution.py:11
  658.0 2.2 maximum_bitcast_fusion
  660.2 5.2 collective-permute-done.6
  665.4 2.3 maximum_bitcast_fusion.1
  667.7 5.7 fusion.6
  673.5 6.0 fusion.8
  679.5 5.8 fusion.7
  (83 shorter events, 6.4 us)
Async XLA Ops:
  7.2 37.1 %all-gather.13.cloned.1.call-start = ((), (), s32[]{:S(2)}) async-start(), calls=%async_computation.2 | async-start | bytes 3096576 | tf_op jit(solution)/shard_map/all_gather | solution.py:78
  11.0 31.3 %copy-start.20 = (u32[128]{0:T(128)S(1)}, u32[128]{0:T(128)}, u32[]{:S(2)}) copy-start(u32[128]{0:T(128)} %constant.32) | copy-start | bytes 1540
  11.8 58.8 %all-gather.9.cloned.1.call-start = ((), (), s32[]{:S(2)}) async-start(), calls=%async_computation | async-start | bytes 3096576 | tf_op jit(solution)/shard_map/all_gather | solution.py:76
  12.6 86.9 %all-gather.15.cloned.1.call-start = ((), (), s32[]{:S(2)}) async-start(), calls=%async_computation.3 | async-start | bytes 3096576 | tf_op jit(solution)/shard_map/all_gather | solution.py:79
  12.7 12.3 %collective-permute-start.5 = (bf16[20,7168]{1,0:T(8,128)(2,1)S(1)}, bf16[20,7168]{1,0:T(8,128)(2,1)S(1)}, u32[]{:S(2)}, u32[]{:S(2)}) collective-permute-start(bf16[20,7168]{1,0:T(8,128)(2,1)S(1)} %get-tuple-element.16), channel_id=1, source_target_pairs={{0,64},{8,72},{16,80},{24,88},{32,96},{40,104},{48,112},{56,120},{... | collective-permute-start | bytes 860168 | tf_op jit(solution)/shard_map/ppermute | solution.py:11
  25.8 102.5 %all-gather.11.cloned.1.call-start = ((), (), s32[]{:S(2)}) async-start(), calls=%async_computation.1 | async-start | bytes 3096576 | tf_op jit(solution)/shard_map/all_gather | solution.py:77
  25.9 10.0 %collective-permute-start = (bf16[20,7168]{1,0:T(8,128)(2,1)S(1)}, bf16[20,7168]{1,0:T(8,128)(2,1)S(1)}, u32[]{:S(2)}, u32[]{:S(2)}) collective-permute-start(bf16[20,7168]{1,0:T(8,128)(2,1)S(1)} %get-tuple-element.18), channel_id=1, source_target_pairs={{0,64},{8,72},{16,80},{24,88},{32,96},{40,104},{48,112},{56,120},{... | collective-permute-start | bytes 860168 | tf_op jit(solution)/shard_map/ppermute | solution.py:11
  36.7 95.8 %collective-permute-start.3 = (bf16[256,7168]{1,0:T(8,128)(2,1)}, bf16[256,7168]{1,0:T(8,128)(2,1)}, u32[]{:S(2)}, u32[]{:S(2)}) collective-permute-start(bf16[256,7168]{1,0:T(8,128)(2,1)} %bitcast.105), channel_id=1, source_target_pairs={{0,64},{8,72},{16,80},{24,88},{32,96},{40,104},{48,112},{56,120},{... | collective-permute-start | bytes 11010056 | tf_op jit(solution)/shard_map/ppermute | solution.py:11
  39.3 156.7 %collective-permute-start.2 = (bf16[7168,256]{1,0:T(8,128)(2,1)}, bf16[7168,256]{1,0:T(8,128)(2,1)}, u32[]{:S(2)}, u32[]{:S(2)}) collective-permute-start(bf16[7168,256]{1,0:T(8,128)(2,1)} %bitcast.104), channel_id=1, source_target_pairs={{0,64},{8,72},{16,80},{24,88},{32,96},{40,104},{48,112},{56,120},{... | collective-permute-start | bytes 11010056 | tf_op jit(solution)/shard_map/ppermute | solution.py:11
  39.8 234.9 %collective-permute-start.1 = (bf16[7168,256]{1,0:T(8,128)(2,1)}, bf16[7168,256]{1,0:T(8,128)(2,1)}, u32[]{:S(2)}, u32[]{:S(2)}) collective-permute-start(bf16[7168,256]{1,0:T(8,128)(2,1)} %bitcast.103), channel_id=1, source_target_pairs={{0,64},{8,72},{16,80},{24,88},{32,96},{40,104},{48,112},{56,120},{... | collective-permute-start | bytes 11010056 | tf_op jit(solution)/shard_map/ppermute | solution.py:11
  73.3 3.1 copy-start.2
  76.5 2.0 copy-start.6
  76.5 2.8 copy-start.8
  80.6 2.2 copy-start.13
  80.6 3.5 copy-start.17
  82.8 2.3 copy-start.4
  132.4 63.6 %copy-start = (bf16[160,7168]{1,0:T(8,128)(2,1)S(1)}, bf16[160,7168]{1,0:T(8,128)(2,1)}, u32[]{:S(2)}) copy-start(bf16[160,7168]{1,0:T(8,128)(2,1)} %reshape.22) | copy-start | bytes 6881284
  132.4 63.6 %copy-start.5 = (bf16[1,7168,256]{2,1,0:T(8,128)(2,1)S(1)}, bf16[1,7168,256]{2,1,0:T(8,128)(2,1)}, u32[]{:S(2)}) copy-start(bf16[1,7168,256]{2,1,0:T(8,128)(2,1)} %param.10) | copy-start | bytes 11010052
  137.6 137.1 %copy-start.3 = (bf16[1,7168,256]{2,1,0:T(8,128)(2,1)S(1)}, bf16[1,7168,256]{2,1,0:T(8,128)(2,1)}, u32[]{:S(2)}) copy-start(bf16[1,7168,256]{2,1,0:T(8,128)(2,1)} %param.9) | copy-start | bytes 11010052
  199.1 78.8 %copy-start.7 = (bf16[1,256,7168]{2,1,0:T(8,128)(2,1)S(1)}, bf16[1,256,7168]{2,1,0:T(8,128)(2,1)}, u32[]{:S(2)}) copy-start(bf16[1,256,7168]{2,1,0:T(8,128)(2,1)} %param.11) | copy-start | bytes 11010052
  277.8 4.7 copy-start.12
  277.8 8.1 %copy-start.15 = (bf16[160,256]{1,0:T(8,128)(2,1)}, bf16[160,256]{1,0:T(8,128)(2,1)S(1)}, u32[]{:S(2)}) copy-start(bf16[160,256]{1,0:T(8,128)(2,1)S(1)} %get-tuple-element.26) | copy-start | bytes 245764
  358.5 15.4 %copy-start.10 = (bf16[24,7168]{1,0:T(8,128)(2,1)}, bf16[24,7168]{1,0:T(8,128)(2,1)S(1)}, u32[]{:S(2)}) copy-start(bf16[24,7168]{1,0:T(8,128)(2,1)S(1)} %get-tuple-element.11) | copy-start | bytes 1032196
  358.6 39.4 %collective-permute-start.12 = (bf16[24,7168]{1,0:T(8,128)(2,1)S(1)}, bf16[24,7168]{1,0:T(8,128)(2,1)S(1)}, u32[]{:S(2)}, u32[]{:S(2)}) collective-permute-start(bf16[24,7168]{1,0:T(8,128)(2,1)S(1)} %get-tuple-element.11), channel_id=1, source_target_pairs={{0,1},{1,2},{2,3},{3,4},{4,5},{5,6},{6,7},{8,9},{9,10},{10,11},{11... | collective-permute-start | bytes 1032200
  364.5 9.4 %copy-start.1 = (bf16[160,7168]{1,0:T(8,128)(2,1)S(1)}, bf16[160,7168]{1,0:T(8,128)(2,1)}, u32[]{:S(2)}) copy-start(bf16[160,7168]{1,0:T(8,128)(2,1)} %reshape.22) | copy-start | bytes 6881284
  364.5 9.4 %copy-start.16 = (bf16[160,256]{1,0:T(8,128)(2,1)S(1)}, bf16[160,256]{1,0:T(8,128)(2,1)}, u32[]{:S(2)}) copy-start(bf16[160,256]{1,0:T(8,128)(2,1)} %copy-done.15) | copy-start | bytes 245764
  364.5 58.8 %collective-permute-start.10 = (bf16[24,7168]{1,0:T(8,128)(2,1)}, bf16[24,7168]{1,0:T(8,128)(2,1)}, u32[]{:S(2)}, u32[]{:S(2)}) collective-permute-start(bf16[24,7168]{1,0:T(8,128)(2,1)} %get-tuple-element.12), channel_id=1, source_target_pairs={{0,1},{1,2},{2,3},{3,4},{4,5},{5,6},{6,7},{8,9},{9,10},{10,11},{11... | collective-permute-start | bytes 1032200
  379.4 16.4 %collective-permute-start.13 = (bf16[4,7168]{1,0:T(4,128)(2,1)S(1)}, bf16[4,7168]{1,0:T(4,128)(2,1)S(1)}, u32[]{:S(2)}, u32[]{:S(2)}) collective-permute-start(bf16[4,7168]{1,0:T(4,128)(2,1)S(1)} %slice.31), channel_id=1, source_target_pairs={{0,2},{1,3},{2,4},{3,5},{4,6},{5,7},{8,10},{9,11},{10,12},{11,13},... | collective-permute-start | bytes 172040
  387.6 23.9 %collective-permute-start.16 = (bf16[24,7168]{1,0:T(8,128)(2,1)}, bf16[24,7168]{1,0:T(8,128)(2,1)}, u32[]{:S(2)}, u32[]{:S(2)}) collective-permute-start(bf16[24,7168]{1,0:T(8,128)(2,1)} %get-tuple-element.13), channel_id=1, source_target_pairs={{0,1},{1,2},{2,3},{3,4},{4,5},{5,6},{6,7},{8,9},{9,10},{10,11},{11... | collective-permute-start | bytes 1032200
  393.1 41.1 %collective-permute-start.14 = (bf16[24,7168]{1,0:T(8,128)(2,1)S(1)}, bf16[24,7168]{1,0:T(8,128)(2,1)}, u32[]{:S(2)}, u32[]{:S(2)}) collective-permute-start(bf16[24,7168]{1,0:T(8,128)(2,1)S(1)} %get-tuple-element.14), channel_id=1, source_target_pairs={{0,1},{1,2},{2,3},{3,4},{4,5},{5,6},{6,7},{8,9},{9,10},{10,11},{11... | collective-permute-start | bytes 1032200
  395.7 2.3 copy-start.19
  395.7 35.6 %collective-permute-start.15 = (bf16[4,7168]{1,0:T(4,128)(2,1)}, bf16[4,7168]{1,0:T(4,128)(2,1)}, u32[]{:S(2)}, u32[]{:S(2)}) collective-permute-start(bf16[4,7168]{1,0:T(4,128)(2,1)} %slice.32), channel_id=1, source_target_pairs={{0,2},{1,3},{2,4},{3,5},{4,6},{5,7},{8,10},{9,11},{10,12},{11,13},... | collective-permute-start | bytes 172040
  398.0 0.7 copy-start.11
  398.7 10.8 %collective-permute-start.17 = (bf16[4,7168]{1,0:T(4,128)(2,1)}, bf16[4,7168]{1,0:T(4,128)(2,1)}, u32[]{:S(2)}, u32[]{:S(2)}) collective-permute-start(bf16[4,7168]{1,0:T(4,128)(2,1)} %slice.33), channel_id=1, source_target_pairs={{0,2},{1,3},{2,4},{3,5},{4,6},{5,7},{8,10},{9,11},{10,12},{11,13},... | collective-permute-start | bytes 172040
  409.5 10.8 %collective-permute-start.11 = (bf16[4,7168]{1,0:T(4,128)(2,1)}, bf16[4,7168]{1,0:T(4,128)(2,1)}, u32[]{:S(2)}, u32[]{:S(2)}) collective-permute-start(bf16[4,7168]{1,0:T(4,128)(2,1)} %slice.30), channel_id=1, source_target_pairs={{0,2},{1,3},{2,4},{3,5},{4,6},{5,7},{8,10},{9,11},{10,12},{11,13},... | collective-permute-start | bytes 172040
  411.5 256.2 %collective-permute-start.9 = (bf16[256,7168]{1,0:T(8,128)(2,1)}, bf16[256,7168]{1,0:T(8,128)(2,1)}, u32[]{:S(2)}, u32[]{:S(2)}) collective-permute-start(bf16[256,7168]{1,0:T(8,128)(2,1)} %get-tuple-element.35), channel_id=1, source_target_pairs={{0,64},{8,72},{16,80},{24,88},{32,96},{40,104},{48,112},{56,120},{... | collective-permute-start | bytes 11010056 | tf_op jit(solution)/shard_map/ppermute | solution.py:11
  420.4 253.1 %collective-permute-start.7 = (bf16[7168,256]{1,0:T(8,128)(2,1)}, bf16[7168,256]{1,0:T(8,128)(2,1)}, u32[]{:S(2)}, u32[]{:S(2)}) collective-permute-start(bf16[7168,256]{1,0:T(8,128)(2,1)} %get-tuple-element.31), channel_id=1, source_target_pairs={{0,64},{8,72},{16,80},{24,88},{32,96},{40,104},{48,112},{56,120},{... | collective-permute-start | bytes 11010056 | tf_op jit(solution)/shard_map/ppermute | solution.py:11
  423.3 256.1 %collective-permute-start.8 = (bf16[7168,256]{1,0:T(8,128)(2,1)}, bf16[7168,256]{1,0:T(8,128)(2,1)}, u32[]{:S(2)}, u32[]{:S(2)}) collective-permute-start(bf16[7168,256]{1,0:T(8,128)(2,1)} %get-tuple-element.33), channel_id=1, source_target_pairs={{0,64},{8,72},{16,80},{24,88},{32,96},{40,104},{48,112},{56,120},{... | collective-permute-start | bytes 11010056 | tf_op jit(solution)/shard_map/ppermute | solution.py:11
  431.3 226.7 %collective-permute-start.4 = (bf16[20,7168]{1,0:T(8,128)(2,1)}, bf16[20,7168]{1,0:T(8,128)(2,1)}, u32[]{:S(2)}, u32[]{:S(2)}) collective-permute-start(bf16[20,7168]{1,0:T(8,128)(2,1)} %get-tuple-element.22), channel_id=1, source_target_pairs={{0,64},{8,72},{16,80},{24,88},{32,96},{40,104},{48,112},{56,120},{... | collective-permute-start | bytes 860168 | tf_op jit(solution)/shard_map/ppermute | solution.py:11
  434.3 231.1 %collective-permute-start.6 = (bf16[20,7168]{1,0:T(8,128)(2,1)}, bf16[20,7168]{1,0:T(8,128)(2,1)}, u32[]{:S(2)}, u32[]{:S(2)}) collective-permute-start(bf16[20,7168]{1,0:T(8,128)(2,1)} %get-tuple-element.20), channel_id=1, source_target_pairs={{0,64},{8,72},{16,80},{24,88},{32,96},{40,104},{48,112},{56,120},{... | collective-permute-start | bytes 860168 | tf_op jit(solution)/shard_map/ppermute | solution.py:11
  444.1 223.6 %copy-start.9 = (bf16[160,7168]{1,0:T(8,128)(2,1)S(1)}, bf16[160,7168]{1,0:T(8,128)(2,1)}, u32[]{:S(2)}) copy-start(bf16[160,7168]{1,0:T(8,128)(2,1)} %reshape.24) | copy-start | bytes 6881284
  665.4 8.1 %slice-start.2 = ((s8[7340032]{0:T(1024)(128)(4,1)}), s8[4194304]{0:T(1024)(128)(4,1)S(1)}, s32[]{:S(2)}) async-start(s8[7340032]{0:T(1024)(128)(4,1)} %bitcast.101), calls=%async_computation.6 | async-start | bytes 8388608
  667.7 5.8 slice-start.3
  667.7 5.8 copy-start.14
  667.7 11.8 %slice-start = ((s8[7340032]{0:T(1024)(128)(4,1)}), s8[4194304]{0:T(1024)(128)(4,1)S(1)}, s32[]{:S(2)}) async-start(s8[7340032]{0:T(1024)(128)(4,1)} %bitcast.99), calls=%async_computation.4 | async-start | bytes 8388608
  673.5 6.0 slice-start.1
  673.5 6.0 copy-start.18
Sparse Core Ops, SparseCore 0:
  11.9 29.6 all-gather.12
  43.9 26.6 all-gather.8
  72.8 26.6 all-gather.14
  101.6 26.6 all-gather.10
where the time goes:
time: 696 us; the launch traced here: 692 us
  waiting for transfers between devices  425 us (61%)
  matrix products  71.3 us (10%)
  blocking collectives  67.5 us (10%)
  local copies, waits for them, and re-layouts  59.5 us (9%)
  starting transfers between devices  40.9 us (6%)
  between operations  15.4 us (2%)
  other arithmetic  12 us (2%)
    ppermute x10, waiting for transfers between devices, swapped(): lax.ppermute(x, axis, [(i, i ^ 1 << distance) for i in range(lax.axis_siz...  367 us
    unnamed x1, blocking collectives  67.5 us
    unnamed x67, local copies, waits for them, and re-layouts  59.5 us
    dot_general x6, matrix products, contract_first(): lax.dot_general(left, right, (((0,), (0,)), ((), ())), preferred_element_...  35.4 us
    all_gather x1, waiting for transfers between devices, shards(): lax.all_gather(region_rows, 'dp', axis=0, tiled=True)  24.7 us
    all_gather x1, waiting for transfers between devices, shards(): lax.all_gather(masked[:border], 'dp', axis=0, tiled=True)  22.2 us
    unnamed x8, starting transfers between devices  21.5 us
    dot_general x6, matrix products, contract_last(): lax.dot_general(left, right, (((1,), (1,)), ((), ())), preferred_element_...  19.2 us
  transfers between devices with their start and end apart: 22, of which 9 were waited for; matrix products, arithmetic and copies ran while one was open for 16% of the time, Pallas kernels for 0%

commit v1 on v0

v1 whole, which is shorter than its diff:
```python
import jax
import jax.numpy as jnp
from jax import lax
from jax.sharding import PartitionSpec as P


def silu_slope(value):
    sigma = jax.nn.sigmoid(value)
    return sigma * (1.0 + value * (1.0 - sigma))


def contract_last(left, right):
    return lax.dot_general(
        left, right, (((1,), (1,)), ((), ())), preferred_element_type=jnp.float32
    )


def contract_first(left, right):
    return lax.dot_general(
        left, right, (((0,), (0,)), ((), ())), preferred_element_type=jnp.float32
    )


def expert_work(rows, cot_rows, gate_w, up_w, down_w):
    gate = jnp.dot(rows, gate_w, preferred_element_type=jnp.float32)
    up = jnp.dot(rows, up_w, preferred_element_type=jnp.float32)
    active = jax.nn.silu(gate)
    hidden = (active * up).astype(jnp.bfloat16)
    out_part = jnp.dot(hidden, down_w, preferred_element_type=jnp.float32)
    hidden_grad = contract_last(cot_rows, down_w)
    gate_act = (hidden_grad * up * silu_slope(gate)).astype(jnp.bfloat16)
    up_act = (hidden_grad * active).astype(jnp.bfloat16)
    in_part = contract_last(gate_act, gate_w) + contract_last(up_act, up_w)
    gate_term = contract_first(rows, gate_act)
    up_term = contract_first(rows, up_act)
    down_term = contract_first(hidden, cot_rows)
    return (out_part, in_part, gate_term, up_term, down_term)


def shards(tokens, cotangent, counts, w_gate, w_up, w_down):
    rows_in = tokens[0]
    cot_in = cotangent[0]
    gate_w = w_gate[0]
    up_w = w_up[0]
    down_w = w_down[0]
    expert_pos = lax.axis_index("expert")
    batch_pos = lax.axis_index("dp")
    expert_ids = jnp.arange(counts.shape[0], dtype=jnp.int32)
    batch_ids = jnp.arange(counts.shape[1], dtype=jnp.int32)
    own_counts = jnp.sum(jnp.where(expert_ids[:, None] == expert_pos, counts, 0), axis=0)
    own_total = jnp.sum(jnp.where(batch_ids == batch_pos, own_counts, 0))
    slots = rows_in.shape[0]
    valid = (jnp.arange(slots, dtype=jnp.int32) < own_total)[:, None]
    masked = jnp.where(valid, rows_in, jnp.zeros_like(rows_in))
    masked_cot = jnp.where(valid, cot_in, jnp.zeros_like(cot_in))
    all_rows = lax.all_gather(masked, "dp", axis=0, tiled=True)
    all_cot = lax.all_gather(masked_cot, "dp", axis=0, tiled=True)
    out_part, in_part, gate_term, up_term, down_term = expert_work(
        all_rows, all_cot, gate_w, up_w, down_w
    )
    outputs = lax.psum_scatter(
        out_part.astype(jnp.bfloat16), "dp", scatter_dimension=0, tiled=True
    )
    input_grads = lax.psum_scatter(
        in_part.astype(jnp.bfloat16), "dp", scatter_dimension=0, tiled=True
    )
    gate_grad = gate_term.astype(jnp.bfloat16)
    up_grad = up_term.astype(jnp.bfloat16)
    down_grad = down_term.astype(jnp.bfloat16)
    return (outputs[None], input_grads[None], gate_grad[None], up_grad[None], down_grad[None])


def solution(mesh):
    placed = (
        P("expert", "dp", None),
        P("expert", "dp", None),
        P(),
        P("expert", None, "dp"),
        P("expert", None, "dp"),
        P("expert", "dp", None),
    )
    return jax.shard_map(
        shards,
        mesh=mesh,
        in_specs=placed,
        out_specs=(
            P("expert", "dp", None),
            P("expert", "dp", None),
            P("expert", None, "dp"),
            P("expert", None, "dp"),
            P("expert", "dp", None),
        ),
        check_vma=False,
    )
```

time: 696 us -> 265 us (0.38)
  waiting for transfers between devices: 425 us -> 77.7 us
  starting transfers between devices: 40.9 us -> 6.38 us
  local copies, waits for them, and re-layouts: 59.5 us -> 26.2 us
  matrix products: 71.3 us -> 51.1 us
  blocking collectives: 67.5 us -> 83.7 us
  other arithmetic: 12 us -> 4.97 us
    ppermute x10 -> x0, waiting for transfers between devices: 367 us -> none  [swapped(): lax.ppermute(x, axis, [(i, i ^ 1 << distance) for i in range(lax.axis_siz...]
    unnamed x67 -> x21, local copies, waits for them, and re-layouts: 59.5 us -> 23.9 us
    dot_general x6 -> x3, matrix products: 35.4 us -> 15 us  [contract_first(): lax.dot_general(left, right, (((0,), (0,)), ((), ())), preferred_element_...]
    ppermute x10 -> x0, starting transfers between devices: 19.2 us -> none  [swapped(): lax.ppermute(x, axis, [(i, i ^ 1 << distance) for i in range(lax.axis_siz...]
    all_gather x4 -> x2, waiting for transfers between devices: 58.5 us -> 77 us  [the longest x1 46.4 us: shards(): all_rows = lax.all_gather(masked, 'dp', axis=0, tiled=True)]
    unnamed x1, blocking collectives: 67.5 us -> 83.7 us
    unnamed x8 -> x2, starting transfers between devices: 21.5 us -> 6.3 us
    dot_general x6 -> x3, matrix products: 19.2 us -> 23.2 us  [contract_last(): lax.dot_general(left, right, (((1,), (1,)), ((), ())), preferred_element_...]
  transfers between devices with their start and end apart: 22 -> 4, of which waited for: 9 -> 2; matrix products, arithmetic and copies ran while one was open for 16% -> 11% of each run, Pallas kernels for 0% -> 0%
where the time goes in v1:
time: 265 us
  blocking collectives  83.7 us (32%)
  waiting for transfers between devices  77.7 us (29%)
  matrix products  51.1 us (19%)
  local copies, waits for them, and re-layouts  26.2 us (10%)
  between operations  14.8 us (6%)
  starting transfers between devices  6.38 us (2%)
  other arithmetic  4.97 us (2%)
    unnamed x1, blocking collectives  83.7 us
    all_gather x1, waiting for transfers between devices, shards(): all_rows = lax.all_gather(masked, 'dp', axis=0, tiled=True)  46.4 us
    all_gather x1, waiting for transfers between devices, shards(): all_cot = lax.all_gather(masked_cot, 'dp', axis=0, tiled=True)  30.6 us
    unnamed x21, local copies, waits for them, and re-layouts  23.9 us
    dot_general x3, matrix products, contract_last(): lax.dot_general(left, right, (((1,), (1,)), ((), ())), preferred_element_...  23.2 us
    dot_general x3, matrix products, contract_first(): lax.dot_general(left, right, (((0,), (0,)), ((), ())), preferred_element_...  15 us
    unnamed x2, starting transfers between devices  6.3 us
    dot_general x1, matrix products, expert_work(): gate = jnp.dot(rows, gate_w, preferred_element_type=jnp.float32)  6.16 us
  transfers between devices with their start and end apart: 4, of which 2 were waited for; matrix products, arithmetic and copies ran while one was open for 11% of the time, Pallas kernels for 0%

profile of v1, /device:TPU:1, one launch (start us, length us, event | category | flops | bytes accessed | tf_op | source)
XLA Modules:
  0.0 264.8 jit_solution(1845619479661166397)
XLA Ops:
  7.2 0.0 all-gather.5.cloned.1.call-start
  7.2 0.8 select_reduce_fusion
  8.0 0.6 fusion.18
  8.7 0.6 iota_compare_fusion.1
  9.3 2.9 %fusion.15 = (bf16[1,60,7168]{2,1,0:T(8,128)(2,1)}, bf16[1,60,7168]{2,1,0:T(8,128)(2,1)}) fusion(bf16[1,60,7168]{2,1,0:T(8,128)(2,1)} %param.7, pred[60]{0:T(512)(128)(4,1)S(1)} %iota_compare_fusion.1, bf16[1,60,7168]{2,1,0:T(8,128)(2,1)} %param.6), kind=kLoop, calls=%fused_computation.21 | loop fusion | flops 860160 | bytes 3440700
  12.2 0.0 all-gather.5.cloned.1.call-update
  12.2 0.0 all-gather.7.cloned.1.call-start
  12.3 0.7 all-gather.7.cloned.1.call-update
  13.0 1.2 dynamic-slice.6
  14.9 46.4 %all-gather.5.cloned.1.call-done = bf16[8,60,7168]{2,1,0:T(8,128)(2,1)} async-done(((bf16[1,60,7168]{2,1,0:T(8,128)(2,1)}), bf16[8,60,7168]{2,1,0:T(8,128)(2,1)}) %all-gather.5.cloned.1.call-update) | async-done | bytes 6881296 | tf_op jit(solution)/shard_map/all_gather | solution.py:56
  61.2 6.9 %reshape.20 = bf16[480,7168]{1,0:T(8,128)(2,1)} reshape(bf16[8,60,7168]{2,1,0:T(8,128)(2,1)} %all-gather.5.cloned.1.call-done) | data formatting | bytes 13762560
  68.2 0.0 copy-start
  68.2 0.0 copy-start.1
  68.2 6.2 %fusion.13 = f32[480,256]{1,0:T(8,128)S(1)} fusion(bf16[480,7168]{1,0:T(8,128)(2,1)} %reshape.20, bf16[1,7168,256]{2,1,0:T(8,128)(2,1)} %param.9), kind=kOutput, calls=%fused_computation.16 | convolution fusion | flops 1761607680 | bytes 11042816 | tf_op jit(solution)/shard_map/dot_general | solution.py:25
  74.3 0.4 copy-done
  74.8 1.6 copy-done.1
  76.4 1.9 fusion.9
  78.3 30.6 %all-gather.7.cloned.1.call-done = bf16[8,60,7168]{2,1,0:T(8,128)(2,1)} async-done(((bf16[1,60,7168]{2,1,0:T(8,128)(2,1)}), bf16[8,60,7168]{2,1,0:T(8,128)(2,1)}) %all-gather.7.cloned.1.call-update) | async-done | bytes 6881296 | tf_op jit(solution)/shard_map/all_gather | solution.py:57
  108.9 6.8 %reshape.22 = bf16[480,7168]{1,0:T(8,128)(2,1)} reshape(bf16[8,60,7168]{2,1,0:T(8,128)(2,1)} %all-gather.7.cloned.1.call-done) | data formatting | bytes 13762560
  115.7 0.0 copy-start.4
  115.7 0.0 slice-start
  115.7 6.2 %multiply_convert_fusion = (bf16[480,256]{1,0:T(8,128)(2,1)S(1)}, bf16[480,256]{1,0:T(8,128)(2,1)S(1)}, bf16[480,256]{1,0:T(8,128)(2,1)S(1)}) fusion(f32[480,256]{1,0:T(8,128)S(1)} %fusion.13, f32[480,256]{1,0:T(8,128)S(1)} %fusion.9, bf16[480,7168]{1,0:T(8,128)(2,1)} %reshape.22, bf16[1,256,7168]{2,1,0:T(8,128)(2,1)} %param.11), kind=kOutput, calls=%fused_computation.24 | convolution fusion | flops 1763450880 | bytes 12271616 | tf_op jit(solution)/shard_map/dot_general | solution.py:13
  121.9 0.0 copy-done.4
  121.9 0.0 slice-start.1
  121.9 6.9 %fusion.11 = f32[480,7168]{1,0:T(8,128)} fusion(bf16[480,256]{1,0:T(8,128)(2,1)S(1)} %get-tuple-element.10, bf16[1,7168,256]{2,1,0:T(8,128)(2,1)S(1)} %copy-done.4), kind=kOutput, calls=%fused_computation.14 | convolution fusion | flops 1761607680 | bytes 17678336 | tf_op jit(solution)/shard_map/dot_general | solution.py:13
  128.9 0.0 slice-done
  128.9 0.0 slice-done.1
  128.9 4.0 %fusion.2 = bf16[1,7168,256]{2,1,0:T(8,128)(2,1)} fusion(bf16[480,7168]{1,0:T(8,128)(2,1)S(1)} %bitcast.58, bf16[480,256]{1,0:T(8,128)(2,1)S(1)} %get-tuple-element.10), kind=kOutput, calls=%fused_computation.5 | convolution fusion | flops 1763442688 | bytes 10797056 | tf_op jit(solution)/shard_map/dot_general | solution.py:19
  132.9 0.0 copy-start.2
  132.9 4.0 %fusion.3 = bf16[1,7168,256]{2,1,0:T(8,128)(2,1)} fusion(bf16[480,7168]{1,0:T(8,128)(2,1)S(1)} %bitcast.58, bf16[480,256]{1,0:T(8,128)(2,1)S(1)} %get-tuple-element.9), kind=kOutput, calls=%fused_computation.6 | convolution fusion | flops 1763442688 | bytes 10797056 | tf_op jit(solution)/shard_map/dot_general | solution.py:19
  137.0 0.0 copy-done.2
  137.0 0.0 copy-start.3
  137.0 10.0 %add_convert_fusion = bf16[480,7168]{1,0:T(8,128)(2,1)} fusion(f32[480,7168]{1,0:T(8,128)} %fusion.11, bf16[480,256]{1,0:T(8,128)(2,1)S(1)} %get-tuple-element.9, bf16[1,7168,256]{2,1,0:T(8,128)(2,1)S(1)} %copy-done.2), kind=kOutput, calls=%fused_computation | convolution fusion | flops 1768488960 | bytes 24559616 | tf_op jit(solution)/shard_map/dot_general | solution.py:13
  147.0 0.0 copy-done.3
  147.0 4.8 %convolution_convert_fusion = bf16[480,7168]{1,0:T(8,128)(2,1)} fusion(bf16[480,256]{1,0:T(8,128)(2,1)S(1)} %get-tuple-element.11, bf16[1,256,7168]{2,1,0:T(8,128)(2,1)S(1)} %copy-done.3), kind=kOutput, calls=%fused_computation.1 | convolution fusion | flops 1765048320 | bytes 10797056 | tf_op jit(solution)/shard_map/dot_general | solution.py:29
  151.8 83.7 %fusion.19 = (bf16[64,7168]{1,0:T(8,128)(2,1)S(1)}, bf16[64,7168]{1,0:T(8,128)(2,1)S(1)}) fusion(bf16[480,7168]{1,0:T(8,128)(2,1)} %convolution_convert_fusion, bf16[480,7168]{1,0:T(8,128)(2,1)} %add_convert_fusion), kind=kCustom, calls=%all-reduce-scatter.2 | all-reduce-scatter fusion | flops 7340033 | bytes 15598080
  235.5 0.1 slice.1
  235.6 4.4 %collective-permute-start.1 = (bf16[28,7168]{1,0:T(8,128)(2,1)S(1)}, bf16[28,7168]{1,0:T(8,128)(2,1)}, u32[]{:S(2)}, u32[]{:S(2)}) collective-permute-start(bf16[28,7168]{1,0:T(8,128)(2,1)S(1)} %slice.1), channel_id=1, source_target_pairs={{0,1},{1,2},{2,3},{3,4},{4,5},{5,6},{6,7},{8,9},{9,10},{10,11},{11... | collective-permute-start | bytes 1204232
  240.0 0.9 slice
  240.9 1.9 collective-permute-start
  242.8 6.9 %fusion.4 = bf16[1,256,7168]{2,1,0:T(8,128)(2,1)} fusion(bf16[480,256]{1,0:T(8,128)(2,1)S(1)} %get-tuple-element.11, bf16[480,7168]{1,0:T(8,128)(2,1)} %reshape.22), kind=kOutput, calls=%fused_computation.7 | convolution fusion | flops 1763442688 | bytes 10797056 | tf_op jit(solution)/shard_map/dot_general | solution.py:19
  249.7 0.0 collective-permute-done.1
  249.7 3.0 %concatenate.1 = bf16[92,7168]{1,0:T(8,128)(2,1)S(1)} concatenate(bf16[28,7168]{1,0:T(8,128)(2,1)} %collective-permute-done.1, bf16[64,7168]{1,0:T(8,128)(2,1)S(1)} %get-tuple-element.8), dimensions={0} | concatenate | bytes 2637824
  252.7 1.2 dynamic-slice_bitcast_fusion
  253.8 0.0 collective-permute-done
  253.8 3.0 %concatenate = bf16[92,7168]{1,0:T(8,128)(2,1)S(1)} concatenate(bf16[28,7168]{1,0:T(8,128)(2,1)} %collective-permute-done, bf16[64,7168]{1,0:T(8,128)(2,1)S(1)} %get-tuple-element.7), dimensions={0} | concatenate | bytes 2637824
  256.8 1.2 dynamic-slice_bitcast_fusion.1
  (2 shorter events, 0.0 us)
Async XLA Ops:
  7.2 54.1 %all-gather.5.cloned.1.call-start = ((), (), s32[]{:S(2)}) async-start(), calls=%async_computation | async-start | bytes 8257536 | tf_op jit(solution)/shard_map/all_gather | solution.py:56
  12.2 96.7 %all-gather.7.cloned.1.call-start = ((), (), s32[]{:S(2)}) async-start(), calls=%async_computation.1 | async-start | bytes 8257536 | tf_op jit(solution)/shard_map/all_gather | solution.py:57
  68.2 6.6 %copy-start = (bf16[480,7168]{1,0:T(8,128)(2,1)S(1)}, bf16[480,7168]{1,0:T(8,128)(2,1)}, u32[]{:S(2)}) copy-start(bf16[480,7168]{1,0:T(8,128)(2,1)} %reshape.20) | copy-start | bytes 20643844
  68.2 8.2 %copy-start.1 = (bf16[1,7168,256]{2,1,0:T(8,128)(2,1)S(1)}, bf16[1,7168,256]{2,1,0:T(8,128)(2,1)}, u32[]{:S(2)}) copy-start(bf16[1,7168,256]{2,1,0:T(8,128)(2,1)} %param.10) | copy-start | bytes 11010052
  115.7 6.2 %copy-start.4 = (bf16[1,7168,256]{2,1,0:T(8,128)(2,1)S(1)}, bf16[1,7168,256]{2,1,0:T(8,128)(2,1)}, u32[]{:S(2)}) copy-start(bf16[1,7168,256]{2,1,0:T(8,128)(2,1)} %param.9) | copy-start | bytes 11010052
  115.7 13.2 %slice-start = ((s8[6881280]{0:T(1024)(128)(4,1)}), s8[4194304]{0:T(1024)(128)(4,1)S(1)}, s32[]{:S(2)}) async-start(s8[6881280]{0:T(1024)(128)(4,1)} %bitcast.57), calls=%async_computation.2 | async-start | bytes 8388608
  121.9 7.0 %slice-start.1 = ((s8[6881280]{0:T(1024)(128)(4,1)}), s8[2686976]{0:T(1024)(128)(4,1)S(1)}, s32[]{:S(2)}) async-start(s8[6881280]{0:T(1024)(128)(4,1)} %bitcast.57), calls=%async_computation.3 | async-start | bytes 5373952
  132.9 4.0 %copy-start.2 = (bf16[1,7168,256]{2,1,0:T(8,128)(2,1)S(1)}, bf16[1,7168,256]{2,1,0:T(8,128)(2,1)}, u32[]{:S(2)}) copy-start(bf16[1,7168,256]{2,1,0:T(8,128)(2,1)} %param.10) | copy-start | bytes 11010052
  137.0 10.0 %copy-start.3 = (bf16[1,256,7168]{2,1,0:T(8,128)(2,1)S(1)}, bf16[1,256,7168]{2,1,0:T(8,128)(2,1)}, u32[]{:S(2)}) copy-start(bf16[1,256,7168]{2,1,0:T(8,128)(2,1)} %param.11) | copy-start | bytes 11010052
  235.6 14.1 %collective-permute-start.1 = (bf16[28,7168]{1,0:T(8,128)(2,1)S(1)}, bf16[28,7168]{1,0:T(8,128)(2,1)}, u32[]{:S(2)}, u32[]{:S(2)}) collective-permute-start(bf16[28,7168]{1,0:T(8,128)(2,1)S(1)} %slice.1), channel_id=1, source_target_pairs={{0,1},{1,2},{2,3},{3,4},{4,5},{5,6},{6,7},{8,9},{9,10},{10,11},{11... | collective-permute-start | bytes 1204232
  240.9 12.9 %collective-permute-start = (bf16[28,7168]{1,0:T(8,128)(2,1)}, bf16[28,7168]{1,0:T(8,128)(2,1)}, u32[]{:S(2)}, u32[]{:S(2)}) collective-permute-start(bf16[28,7168]{1,0:T(8,128)(2,1)} %slice), channel_id=1, source_target_pairs={{0,1},{1,2},{2,3},{3,4},{4,5},{5,6},{6,7},{8,9},{9,10},{10,11},{11... | collective-permute-start | bytes 1204232
Sparse Core Ops, SparseCore 0:
  12.3 48.8 all-gather.4
  63.5 45.3 all-gather.6

commit v2 on v1

--- a/solution.py
+++ b/solution.py
@@ -58,11 +58,12 @@
     out_part, in_part, gate_term, up_term, down_term = expert_work(
         all_rows, all_cot, gate_w, up_w, down_w
     )
+    groups = lax.axis_size("dp")
     outputs = lax.psum_scatter(
-        out_part.astype(jnp.bfloat16), "dp", scatter_dimension=0, tiled=True
+        out_part.astype(jnp.bfloat16).reshape(groups, slots, -1), "dp", scatter_dimension=0, tiled=False
     )
     input_grads = lax.psum_scatter(
-        in_part.astype(jnp.bfloat16), "dp", scatter_dimension=0, tiled=True
+        in_part.astype(jnp.bfloat16).reshape(groups, slots, -1), "dp", scatter_dimension=0, tiled=False
     )
     gate_grad = gate_term.astype(jnp.bfloat16)
     up_grad = up_term.astype(jnp.bfloat16)

time: 265 us -> 237 us (0.89)
  blocking collectives: 83.7 us -> 0 us
  waiting for transfers between devices: 77.7 us -> 135 us
  starting transfers between devices: 6.38 us -> 0.34 us
  local copies, waits for them, and re-layouts: 26.2 us -> 29.5 us
    unnamed x1 -> x0, blocking collectives: 83.7 us -> none
    reduce_scatter x0 -> x2, waiting for transfers between devices: none -> 55 us  [the longest x1 50 us: shards(): lax.psum_scatter(in_part.astype(jnp.bfloat16).reshape(groups, slots, -1),...]
    reshape x0 -> x2, local copies, waits for them, and re-layouts: none -> 13.8 us  [the longest x1 6.96 us: shards(): in_part.astype(jnp.bfloat16).reshape(groups, slots, -1)]
    unnamed x21 -> x14, local copies, waits for them, and re-layouts: 23.9 us -> 15.8 us
    unnamed x2 -> x0, starting transfers between devices: 6.3 us -> none
    dot_general x1, matrix products: 1.94 us -> 6.16 us  [expert_work(): up = jnp.dot(rows, up_w, preferred_element_type=jnp.float32)]
    dot_general x1, matrix products: 6.16 us -> 1.93 us  [expert_work(): gate = jnp.dot(rows, gate_w, preferred_element_type=jnp.float32)]
  transfers between devices with their start and end apart: 4 -> 4, of which waited for: 2 -> 4; matrix products, arithmetic and copies ran while one was open for 11% -> 24% of each run, Pallas kernels for 0% -> 0%
where the time goes in v2:
time: 237 us
  waiting for transfers between devices  135 us (57%)
  matrix products  53.6 us (23%)
  local copies, waits for them, and re-layouts  29.5 us (12%)
  between operations  13.8 us (6%)
  other arithmetic  4.97 us (2%)
    reduce_scatter x1, waiting for transfers between devices, shards(): lax.psum_scatter(in_part.astype(jnp.bfloat16).reshape(groups, slots, -1),...  50 us
    all_gather x1, waiting for transfers between devices, shards(): all_rows = lax.all_gather(masked, 'dp', axis=0, tiled=True)  48.2 us
    all_gather x1, waiting for transfers between devices, shards(): all_cot = lax.all_gather(masked_cot, 'dp', axis=0, tiled=True)  30.6 us
    dot_general x3, matrix products, contract_last(): lax.dot_general(left, right, (((1,), (1,)), ((), ())), preferred_element_...  25.4 us
    unnamed x14, local copies, waits for them, and re-layouts  15.8 us
    dot_general x3, matrix products, contract_first(): lax.dot_general(left, right, (((0,), (0,)), ((), ())), preferred_element_...  15.3 us
    reshape x1, local copies, waits for them, and re-layouts, shards(): in_part.astype(jnp.bfloat16).reshape(groups, slots, -1)  6.96 us
    reshape x1, local copies, waits for them, and re-layouts, shards(): out_part.astype(jnp.bfloat16).reshape(groups, slots, -1)  6.81 us
  transfers between devices with their start and end apart: 4, of which 4 were waited for; matrix products, arithmetic and copies ran while one was open for 24% of the time, Pallas kernels for 0%

profile of v2, /device:TPU:1, one launch (start us, length us, event | category | flops | bytes accessed | tf_op | source)
XLA Modules:
  0.0 236.8 jit_solution(2020578881558079504)
XLA Ops:
  7.2 0.0 all-gather.5.cloned.1.call-start
  7.2 0.8 select_reduce_fusion
  8.0 0.6 fusion.16
  8.7 0.6 iota_compare_fusion.1
  9.3 2.9 %fusion.13 = (bf16[1,60,7168]{2,1,0:T(8,128)(2,1)}, bf16[1,60,7168]{2,1,0:T(8,128)(2,1)}) fusion(bf16[1,60,7168]{2,1,0:T(8,128)(2,1)} %param.7, pred[60]{0:T(512)(128)(4,1)S(1)} %iota_compare_fusion.1, bf16[1,60,7168]{2,1,0:T(8,128)(2,1)} %param.6), kind=kLoop, calls=%fused_computation.19 | loop fusion | flops 860160 | bytes 3440700
  12.2 0.0 all-gather.5.cloned.1.call-update
  12.2 0.0 all-gather.7.cloned.1.call-start
  12.3 0.7 all-gather.7.cloned.1.call-update
  13.0 0.0 reduce-scatter.3.cloned.1.call-start
  13.0 48.2 %all-gather.5.cloned.1.call-done = bf16[8,60,7168]{2,1,0:T(8,128)(2,1)} async-done(((bf16[1,60,7168]{2,1,0:T(8,128)(2,1)}), bf16[8,60,7168]{2,1,0:T(8,128)(2,1)}) %all-gather.5.cloned.1.call-update) | async-done | bytes 6881296 | tf_op jit(solution)/shard_map/all_gather | solution.py:56
  61.3 6.9 %reshape.28 = bf16[480,7168]{1,0:T(8,128)(2,1)} reshape(bf16[8,60,7168]{2,1,0:T(8,128)(2,1)} %all-gather.5.cloned.1.call-done) | data formatting | bytes 13762560
  68.2 0.0 copy-start
  68.2 0.0 copy-start.3
  68.2 6.2 %fusion.7 = f32[480,256]{1,0:T(8,128)S(1)} fusion(bf16[480,7168]{1,0:T(8,128)(2,1)} %reshape.28, bf16[1,7168,256]{2,1,0:T(8,128)(2,1)} %param.10), kind=kOutput, calls=%fused_computation.12 | convolution fusion | flops 1761607680 | bytes 11042816 | tf_op jit(solution)/shard_map/dot_general | solution.py:26
  74.3 0.4 copy-done
  74.8 1.6 copy-done.3
  76.4 1.9 fusion.11
  78.3 30.6 %all-gather.7.cloned.1.call-done = bf16[8,60,7168]{2,1,0:T(8,128)(2,1)} async-done(((bf16[1,60,7168]{2,1,0:T(8,128)(2,1)}), bf16[8,60,7168]{2,1,0:T(8,128)(2,1)}) %all-gather.7.cloned.1.call-update) | async-done | bytes 6881296 | tf_op jit(solution)/shard_map/all_gather | solution.py:57
  108.9 6.8 %reshape.30 = bf16[480,7168]{1,0:T(8,128)(2,1)} reshape(bf16[8,60,7168]{2,1,0:T(8,128)(2,1)} %all-gather.7.cloned.1.call-done) | data formatting | bytes 13762560
  115.7 0.0 copy-start.2
  115.7 6.2 %multiply_convert_fusion = (bf16[480,256]{1,0:T(8,128)(2,1)S(1)}, bf16[480,256]{1,0:T(8,128)(2,1)S(1)}, bf16[480,256]{1,0:T(8,128)(2,1)S(1)}) fusion(f32[480,256]{1,0:T(8,128)S(1)} %fusion.11, f32[480,256]{1,0:T(8,128)S(1)} %fusion.7, bf16[480,7168]{1,0:T(8,128)(2,1)} %reshape.30, bf16[1,256,7168]{2,1,0:T(8,128)(2,1)} %param.11), kind=kOutput, calls=%fused_computation.22 | convolution fusion | flops 1763450880 | bytes 12271616 | tf_op jit(solution)/shard_map/dot_general | solution.py:13
  121.9 0.0 copy-done.2
  121.9 4.8 %convolution_convert_fusion = bf16[480,7168]{1,0:T(8,128)(2,1)} fusion(bf16[480,256]{1,0:T(8,128)(2,1)S(1)} %get-tuple-element.7, bf16[1,256,7168]{2,1,0:T(8,128)(2,1)S(1)} %copy-done.2), kind=kOutput, calls=%fused_computation.1 | convolution fusion | flops 1765048320 | bytes 10797056 | tf_op jit(solution)/shard_map/dot_general | solution.py:29
  126.7 6.8 %reshape.25 = bf16[8,60,7168]{2,1,0:T(8,128)(2,1)} reshape(bf16[480,7168]{1,0:T(8,128)(2,1)} %convolution_convert_fusion) | data formatting | bytes 13762560 | tf_op jit(solution)/shard_map/reshape | solution.py:63
  133.6 0.0 reduce-scatter.3.cloned.1.call-update
  133.6 0.2 reduce-scatter.5.cloned.1.call-start
  133.8 0.0 copy-start.1
  133.8 9.4 %fusion.9 = f32[480,7168]{1,0:T(8,128)} fusion(bf16[480,256]{1,0:T(8,128)(2,1)S(1)} %get-tuple-element.6, bf16[1,7168,256]{2,1,0:T(8,128)(2,1)} %param.9), kind=kOutput, calls=%fused_computation.14 | convolution fusion | flops 1761607680 | bytes 17678336 | tf_op jit(solution)/shard_map/dot_general | solution.py:13
  143.2 0.0 copy-done.1
  143.2 9.8 %add_convert_fusion = bf16[480,7168]{1,0:T(8,128)(2,1)} fusion(f32[480,7168]{1,0:T(8,128)} %fusion.9, bf16[480,256]{1,0:T(8,128)(2,1)S(1)} %get-tuple-element.5, bf16[1,7168,256]{2,1,0:T(8,128)(2,1)S(1)} %copy-done.1), kind=kOutput, calls=%fused_computation | convolution fusion | flops 1768488960 | bytes 24559616 | tf_op jit(solution)/shard_map/dot_general | solution.py:13
  153.0 7.0 %reshape.26 = bf16[8,60,7168]{2,1,0:T(8,128)(2,1)} reshape(bf16[480,7168]{1,0:T(8,128)(2,1)} %add_convert_fusion) | data formatting | bytes 13762560 | tf_op jit(solution)/shard_map/reshape | solution.py:66
  160.0 0.0 slice-start
  160.0 0.0 reduce-scatter.5.cloned.1.call-update
  160.0 0.0 slice-start.1
  160.0 7.2 %fusion.2 = bf16[1,256,7168]{2,1,0:T(8,128)(2,1)} fusion(bf16[480,256]{1,0:T(8,128)(2,1)S(1)} %get-tuple-element.7, bf16[480,7168]{1,0:T(8,128)(2,1)} %reshape.30), kind=kOutput, calls=%fused_computation.7 | convolution fusion | flops 1763442688 | bytes 10797056 | tf_op jit(solution)/shard_map/dot_general | solution.py:19
  167.2 0.0 slice-done
  167.2 0.0 slice-done.1
  167.2 4.0 %fusion.1 = bf16[1,7168,256]{2,1,0:T(8,128)(2,1)} fusion(bf16[480,7168]{1,0:T(8,128)(2,1)S(1)} %bitcast.48, bf16[480,256]{1,0:T(8,128)(2,1)S(1)} %get-tuple-element.5), kind=kOutput, calls=%fused_computation.6 | convolution fusion | flops 1763442688 | bytes 10797056 | tf_op jit(solution)/shard_map/dot_general | solution.py:19
  171.3 4.0 %fusion = bf16[1,7168,256]{2,1,0:T(8,128)(2,1)} fusion(bf16[480,7168]{1,0:T(8,128)(2,1)S(1)} %bitcast.48, bf16[480,256]{1,0:T(8,128)(2,1)S(1)} %get-tuple-element.6), kind=kOutput, calls=%fused_computation.5 | convolution fusion | flops 1763442688 | bytes 10797056 | tf_op jit(solution)/shard_map/dot_general | solution.py:19
  175.3 5.1 %reduce-scatter.3.cloned.1.call-done = bf16[1,60,7168]{2,1,0:T(8,128)(2,1)} async-done(((bf16[8,60,7168]{2,1,0:T(8,128)(2,1)}), bf16[1,60,7168]{2,1,0:T(8,128)(2,1)}) %reduce-scatter.3.cloned.1.call-update) | async-done | bytes 860176 | tf_op jit(solution)/shard_map/reduce_scatter | solution.py:62
  180.4 50.0 %reduce-scatter.5.cloned.1.call-done = bf16[1,60,7168]{2,1,0:T(8,128)(2,1)} async-done(((bf16[8,60,7168]{2,1,0:T(8,128)(2,1)}), bf16[1,60,7168]{2,1,0:T(8,128)(2,1)}) %reduce-scatter.5.cloned.1.call-update) | async-done | bytes 860176 | tf_op jit(solution)/shard_map/reduce_scatter | solution.py:65
  (2 shorter events, 0.0 us)
Async XLA Ops:
  7.2 54.1 %all-gather.5.cloned.1.call-start = ((), (), s32[]{:S(2)}) async-start(), calls=%async_computation.4 | async-start | bytes 8257536 | tf_op jit(solution)/shard_map/all_gather | solution.py:56
  12.2 96.7 %all-gather.7.cloned.1.call-start = ((), (), s32[]{:S(2)}) async-start(), calls=%async_computation.5 | async-start | bytes 8257536 | tf_op jit(solution)/shard_map/all_gather | solution.py:57
  13.0 167.4 %reduce-scatter.3.cloned.1.call-start = ((), (), s32[]{:S(2)}) async-start(), calls=%async_computation.2 | async-start | bytes 8257536 | tf_op jit(solution)/shard_map/reduce_scatter | solution.py:62
  68.2 6.6 %copy-start = (bf16[480,7168]{1,0:T(8,128)(2,1)S(1)}, bf16[480,7168]{1,0:T(8,128)(2,1)}, u32[]{:S(2)}) copy-start(bf16[480,7168]{1,0:T(8,128)(2,1)} %reshape.28) | copy-start | bytes 20643844
  68.2 8.2 %copy-start.3 = (bf16[1,7168,256]{2,1,0:T(8,128)(2,1)S(1)}, bf16[1,7168,256]{2,1,0:T(8,128)(2,1)}, u32[]{:S(2)}) copy-start(bf16[1,7168,256]{2,1,0:T(8,128)(2,1)} %param.9) | copy-start | bytes 11010052
  115.7 6.2 %copy-start.2 = (bf16[1,256,7168]{2,1,0:T(8,128)(2,1)S(1)}, bf16[1,256,7168]{2,1,0:T(8,128)(2,1)}, u32[]{:S(2)}) copy-start(bf16[1,256,7168]{2,1,0:T(8,128)(2,1)} %param.11) | copy-start | bytes 11010052
  133.6 96.7 %reduce-scatter.5.cloned.1.call-start = ((), (), s32[]{:S(2)}) async-start(), calls=%async_computation.3 | async-start | bytes 8257536 | tf_op jit(solution)/shard_map/reduce_scatter | solution.py:65
  133.8 9.4 %copy-start.1 = (bf16[1,7168,256]{2,1,0:T(8,128)(2,1)S(1)}, bf16[1,7168,256]{2,1,0:T(8,128)(2,1)}, u32[]{:S(2)}) copy-start(bf16[1,7168,256]{2,1,0:T(8,128)(2,1)} %param.10) | copy-start | bytes 11010052
  160.0 7.2 %slice-start = ((s8[6881280]{0:T(1024)(128)(4,1)}), s8[2686976]{0:T(1024)(128)(4,1)S(1)}, s32[]{:S(2)}) async-start(s8[6881280]{0:T(1024)(128)(4,1)} %bitcast.47), calls=%async_computation.6 | async-start | bytes 5373952
  160.0 7.2 %slice-start.1 = ((s8[6881280]{0:T(1024)(128)(4,1)}), s8[4194304]{0:T(1024)(128)(4,1)S(1)}, s32[]{:S(2)}) async-start(s8[6881280]{0:T(1024)(128)(4,1)} %bitcast.47), calls=%async_computation.7 | async-start | bytes 8388608
Sparse Core Ops, SparseCore 0:
  12.3 48.8 all-gather.4
  63.5 45.3 all-gather.6
  133.7 46.6 reduce-scatter.2
  183.2 47.0 reduce-scatter.4

commit v3 on v2

--- a/solution.py
+++ b/solution.py
@@ -26,7 +26,9 @@
     up = jnp.dot(rows, up_w, preferred_element_type=jnp.float32)
     active = jax.nn.silu(gate)
     hidden = (active * up).astype(jnp.bfloat16)
-    out_part = jnp.dot(hidden, down_w, preferred_element_type=jnp.float32)
+    out_part = jnp.dot(hidden, down_w, preferred_element_type=jnp.float32).astype(jnp.bfloat16)
+    out_part, hidden, gate, up = lax.optimization_barrier((out_part, hidden, gate, up))
+    active = jax.nn.silu(gate)
     hidden_grad = contract_last(cot_rows, down_w)
     gate_act = (hidden_grad * up * silu_slope(gate)).astype(jnp.bfloat16)
     up_act = (hidden_grad * active).astype(jnp.bfloat16)
@@ -60,7 +62,7 @@
     )
     groups = lax.axis_size("dp")
     outputs = lax.psum_scatter(
-        out_part.astype(jnp.bfloat16).reshape(groups, slots, -1), "dp", scatter_dimension=0, tiled=False
+        out_part.reshape(groups, slots, -1), "dp", scatter_dimension=0, tiled=False
     )
     input_grads = lax.psum_scatter(
         in_part.astype(jnp.bfloat16).reshape(groups, slots, -1), "dp", scatter_dimension=0, tiled=False

time: 237 us -> 215 us (0.907)
  waiting for transfers between devices: 135 us -> 115 us
    all_gather x1, waiting for transfers between devices: 30.6 us -> 18.5 us  [shards(): all_cot = lax.all_gather(masked_cot, 'dp', axis=0, tiled=True)]
    reduce_scatter x1, waiting for transfers between devices: 5.06 us -> 0.01 us  [shards(): lax.psum_scatter(out_part.reshape(groups, slots, -1), 'dp', scatter_dimen...]
    dot_general x1, matrix products: 1.93 us -> 6.16 us  [expert_work(): gate = jnp.dot(rows, gate_w, preferred_element_type=jnp.float32)]
    dot_general x1, matrix products: 6.16 us -> 1.94 us  [expert_work(): up = jnp.dot(rows, up_w, preferred_element_type=jnp.float32)]
    reduce_scatter x1, waiting for transfers between devices: 50 us -> 47.4 us  [shards(): lax.psum_scatter(in_part.astype(jnp.bfloat16).reshape(groups, slots, -1),...]
    unnamed x14 -> x16, local copies, waits for them, and re-layouts: 15.8 us -> 15.9 us
  transfers between devices with their start and end apart: 4 -> 4, of which waited for: 4 -> 3; matrix products, arithmetic and copies ran while one was open for 24% -> 37% of each run, Pallas kernels for 0% -> 0%
where the time goes in v3:
time: 215 us
  waiting for transfers between devices  115 us (53%)
  matrix products  51.3 us (24%)
  local copies, waits for them, and re-layouts  29.7 us (14%)
  between operations  13.8 us (6%)
  other arithmetic  4.97 us (2%)
    all_gather x1, waiting for transfers between devices, shards(): all_rows = lax.all_gather(masked, 'dp', axis=0, tiled=True)  48.2 us
    reduce_scatter x1, waiting for transfers between devices, shards(): lax.psum_scatter(in_part.astype(jnp.bfloat16).reshape(groups, slots, -1),...  47.4 us
    dot_general x3, matrix products, contract_last(): lax.dot_general(left, right, (((1,), (1,)), ((), ())), preferred_element_...  23.2 us
    all_gather x1, waiting for transfers between devices, shards(): all_cot = lax.all_gather(masked_cot, 'dp', axis=0, tiled=True)  18.5 us
    unnamed x16, local copies, waits for them, and re-layouts  15.9 us
    dot_general x3, matrix products, contract_first(): lax.dot_general(left, right, (((0,), (0,)), ((), ())), preferred_element_...  15.2 us
    reshape x1, local copies, waits for them, and re-layouts, shards(): in_part.astype(jnp.bfloat16).reshape(groups, slots, -1)  6.95 us
    reshape x1, local copies, waits for them, and re-layouts, shards(): out_part.reshape(groups, slots, -1)  6.9 us
  transfers between devices with their start and end apart: 4, of which 3 were waited for; matrix products, arithmetic and copies ran while one was open for 37% of the time, Pallas kernels for 0%

profile of v3, /device:TPU:1, one launch (start us, length us, event | category | flops | bytes accessed | tf_op | source)
XLA Modules:
  0.0 215.1 jit_solution(16203403560469040614)
XLA Ops:
  7.2 0.0 all-gather.5.cloned.1.call-start
  7.2 0.8 select_reduce_fusion
  8.0 0.6 fusion.15
  8.7 0.6 iota_compare_fusion.1
  9.3 2.9 %fusion.13 = (bf16[1,60,7168]{2,1,0:T(8,128)(2,1)}, bf16[1,60,7168]{2,1,0:T(8,128)(2,1)}) fusion(bf16[1,60,7168]{2,1,0:T(8,128)(2,1)} %param.7, pred[60]{0:T(512)(128)(4,1)S(1)} %iota_compare_fusion.1, bf16[1,60,7168]{2,1,0:T(8,128)(2,1)} %param.6), kind=kLoop, calls=%fused_computation.19 | loop fusion | flops 860160 | bytes 3440700
  12.2 0.0 all-gather.5.cloned.1.call-update
  12.2 0.0 all-gather.7.cloned.1.call-start
  12.3 0.7 all-gather.7.cloned.1.call-update
  13.0 0.0 reduce-scatter.3.cloned.1.call-start
  13.0 48.2 %all-gather.5.cloned.1.call-done = bf16[8,60,7168]{2,1,0:T(8,128)(2,1)} async-done(((bf16[1,60,7168]{2,1,0:T(8,128)(2,1)}), bf16[8,60,7168]{2,1,0:T(8,128)(2,1)}) %all-gather.5.cloned.1.call-update) | async-done | bytes 6881296 | tf_op jit(solution)/shard_map/all_gather | solution.py:58
  61.3 6.9 %reshape.28 = bf16[480,7168]{1,0:T(8,128)(2,1)} reshape(bf16[8,60,7168]{2,1,0:T(8,128)(2,1)} %all-gather.5.cloned.1.call-done) | data formatting | bytes 13762560
  68.2 0.0 copy-start
  68.2 0.0 copy-start.1
  68.2 6.2 %fusion.11 = f32[480,256]{1,0:T(8,128)S(1)} fusion(bf16[480,7168]{1,0:T(8,128)(2,1)} %reshape.28, bf16[1,7168,256]{2,1,0:T(8,128)(2,1)} %param.9), kind=kOutput, calls=%fused_computation.16 | convolution fusion | flops 1761607680 | bytes 11042816 | tf_op jit(solution)/shard_map/dot_general | solution.py:25
  74.3 0.4 copy-done
  74.8 1.6 copy-done.1
  76.4 0.0 copy-start.3
  76.4 1.9 multiply_convert_fusion.2
  78.4 0.1 copy-done.3
  78.4 4.8 %convolution_convert_fusion = bf16[480,7168]{1,0:T(8,128)(2,1)} fusion(bf16[480,256]{1,0:T(8,128)(2,1)S(1)} %get-tuple-element.12, bf16[1,256,7168]{2,1,0:T(8,128)(2,1)S(1)} %copy-done.3), kind=kOutput, calls=%fused_computation.1 | convolution fusion | flops 1765048320 | bytes 10797056 | tf_op jit(solution)/shard_map/dot_general | solution.py:29
  83.2 6.9 %reshape.25 = bf16[8,60,7168]{2,1,0:T(8,128)(2,1)} reshape(bf16[480,7168]{1,0:T(8,128)(2,1)} %convolution_convert_fusion) | data formatting | bytes 13762560 | tf_op jit(solution)/shard_map/reshape | solution.py:65
  90.1 0.0 reduce-scatter.3.cloned.1.call-update
  90.2 0.2 reduce-scatter.5.cloned.1.call-start
  90.4 18.5 %all-gather.7.cloned.1.call-done = bf16[8,60,7168]{2,1,0:T(8,128)(2,1)} async-done(((bf16[1,60,7168]{2,1,0:T(8,128)(2,1)}), bf16[8,60,7168]{2,1,0:T(8,128)(2,1)}) %all-gather.7.cloned.1.call-update) | async-done | bytes 6881296 | tf_op jit(solution)/shard_map/all_gather | solution.py:59
  108.9 6.8 %reshape.30 = bf16[480,7168]{1,0:T(8,128)(2,1)} reshape(bf16[8,60,7168]{2,1,0:T(8,128)(2,1)} %all-gather.7.cloned.1.call-done) | data formatting | bytes 13762560
  115.7 0.0 copy-start.4
  115.7 6.2 %multiply_convert_fusion = (bf16[480,256]{1,0:T(8,128)(2,1)S(1)}, bf16[480,256]{1,0:T(8,128)(2,1)S(1)}) fusion(f32[480,256]{1,0:T(8,128)S(1)} %fusion.11, f32[480,256]{1,0:T(8,128)S(1)} %get-tuple-element.10, bf16[480,7168]{1,0:T(8,128)(2,1)} %reshape.30, bf16[1,256,7168]{2,1,0:T(8,128)(2,1)} %param.11), kind=kOutput, calls=%fused_computation.22 | convolution fusion | flops 1763205120 | bytes 12025856 | tf_op jit(solution)/shard_map/dot_general | solution.py:13
  121.9 0.0 copy-done.4
  121.9 0.0 copy-start.2
  121.9 6.9 %fusion.9 = f32[480,7168]{1,0:T(8,128)} fusion(bf16[480,256]{1,0:T(8,128)(2,1)S(1)} %get-tuple-element.14, bf16[1,7168,256]{2,1,0:T(8,128)(2,1)S(1)} %copy-done.4), kind=kOutput, calls=%fused_computation.14 | convolution fusion | flops 1761607680 | bytes 17678336 | tf_op jit(solution)/shard_map/dot_general | solution.py:13
  128.8 0.0 copy-done.2
  128.8 10.0 %add_convert_fusion = bf16[480,7168]{1,0:T(8,128)(2,1)} fusion(f32[480,7168]{1,0:T(8,128)} %fusion.9, bf16[480,256]{1,0:T(8,128)(2,1)S(1)} %get-tuple-element.13, bf16[1,7168,256]{2,1,0:T(8,128)(2,1)S(1)} %copy-done.2), kind=kOutput, calls=%fused_computation | convolution fusion | flops 1768488960 | bytes 24559616 | tf_op jit(solution)/shard_map/dot_general | solution.py:13
  138.9 7.0 %reshape.26 = bf16[8,60,7168]{2,1,0:T(8,128)(2,1)} reshape(bf16[480,7168]{1,0:T(8,128)(2,1)} %add_convert_fusion) | data formatting | bytes 13762560 | tf_op jit(solution)/shard_map/reshape | solution.py:68
  145.8 0.0 slice-start
  145.8 0.0 reduce-scatter.5.cloned.1.call-update
  145.9 0.0 slice-start.1
  145.9 7.2 %fusion.2 = bf16[1,256,7168]{2,1,0:T(8,128)(2,1)} fusion(bf16[480,256]{1,0:T(8,128)(2,1)S(1)} %get-tuple-element.12, bf16[480,7168]{1,0:T(8,128)(2,1)} %reshape.30), kind=kOutput, calls=%fused_computation.7 | convolution fusion | flops 1763442688 | bytes 10797056 | tf_op jit(solution)/shard_map/dot_general | solution.py:19
  153.1 0.0 slice-done
  153.1 0.0 slice-done.1
  153.1 4.0 %fusion.1 = bf16[1,7168,256]{2,1,0:T(8,128)(2,1)} fusion(bf16[480,7168]{1,0:T(8,128)(2,1)S(1)} %bitcast.50, bf16[480,256]{1,0:T(8,128)(2,1)S(1)} %get-tuple-element.13), kind=kOutput, calls=%fused_computation.6 | convolution fusion | flops 1763442688 | bytes 10797056 | tf_op jit(solution)/shard_map/dot_general | solution.py:19
  157.1 4.0 %fusion = bf16[1,7168,256]{2,1,0:T(8,128)(2,1)} fusion(bf16[480,7168]{1,0:T(8,128)(2,1)S(1)} %bitcast.50, bf16[480,256]{1,0:T(8,128)(2,1)S(1)} %get-tuple-element.14), kind=kOutput, calls=%fused_computation.5 | convolution fusion | flops 1763442688 | bytes 10797056 | tf_op jit(solution)/shard_map/dot_general | solution.py:19
  161.1 0.0 reduce-scatter.3.cloned.1.call-done
  161.1 47.4 %reduce-scatter.5.cloned.1.call-done = bf16[1,60,7168]{2,1,0:T(8,128)(2,1)} async-done(((bf16[8,60,7168]{2,1,0:T(8,128)(2,1)}), bf16[1,60,7168]{2,1,0:T(8,128)(2,1)}) %reduce-scatter.5.cloned.1.call-update) | async-done | bytes 860176 | tf_op jit(solution)/shard_map/reduce_scatter | solution.py:67
  (2 shorter events, 0.0 us)
Async XLA Ops:
  7.2 54.1 %all-gather.5.cloned.1.call-start = ((), (), s32[]{:S(2)}) async-start(), calls=%async_computation.4 | async-start | bytes 8257536 | tf_op jit(solution)/shard_map/all_gather | solution.py:58
  12.2 96.7 %all-gather.7.cloned.1.call-start = ((), (), s32[]{:S(2)}) async-start(), calls=%async_computation.5 | async-start | bytes 8257536 | tf_op jit(solution)/shard_map/all_gather | solution.py:59
  13.0 148.2 %reduce-scatter.3.cloned.1.call-start = ((), (), s32[]{:S(2)}) async-start(), calls=%async_computation.2 | async-start | bytes 8257536 | tf_op jit(solution)/shard_map/reduce_scatter | solution.py:64
  68.2 6.6 %copy-start = (bf16[480,7168]{1,0:T(8,128)(2,1)S(1)}, bf16[480,7168]{1,0:T(8,128)(2,1)}, u32[]{:S(2)}) copy-start(bf16[480,7168]{1,0:T(8,128)(2,1)} %reshape.28) | copy-start | bytes 20643844
  68.2 8.2 %copy-start.1 = (bf16[1,7168,256]{2,1,0:T(8,128)(2,1)S(1)}, bf16[1,7168,256]{2,1,0:T(8,128)(2,1)}, u32[]{:S(2)}) copy-start(bf16[1,7168,256]{2,1,0:T(8,128)(2,1)} %param.10) | copy-start | bytes 11010052
  76.4 2.0 copy-start.3
  90.2 118.4 %reduce-scatter.5.cloned.1.call-start = ((), (), s32[]{:S(2)}) async-start(), calls=%async_computation.3 | async-start | bytes 8257536 | tf_op jit(solution)/shard_map/reduce_scatter | solution.py:67
  115.7 6.2 %copy-start.4 = (bf16[1,7168,256]{2,1,0:T(8,128)(2,1)S(1)}, bf16[1,7168,256]{2,1,0:T(8,128)(2,1)}, u32[]{:S(2)}) copy-start(bf16[1,7168,256]{2,1,0:T(8,128)(2,1)} %param.9) | copy-start | bytes 11010052
  121.9 7.0 %copy-start.2 = (bf16[1,7168,256]{2,1,0:T(8,128)(2,1)S(1)}, bf16[1,7168,256]{2,1,0:T(8,128)(2,1)}, u32[]{:S(2)}) copy-start(bf16[1,7168,256]{2,1,0:T(8,128)(2,1)} %param.10) | copy-start | bytes 11010052
  145.8 7.2 %slice-start = ((s8[6881280]{0:T(1024)(128)(4,1)}), s8[2686976]{0:T(1024)(128)(4,1)S(1)}, s32[]{:S(2)}) async-start(s8[6881280]{0:T(1024)(128)(4,1)} %bitcast.49), calls=%async_computation.6 | async-start | bytes 5373952
  145.9 7.2 %slice-start.1 = ((s8[6881280]{0:T(1024)(128)(4,1)}), s8[4194304]{0:T(1024)(128)(4,1)S(1)}, s32[]{:S(2)}) async-start(s8[6881280]{0:T(1024)(128)(4,1)} %bitcast.49), calls=%async_computation.7 | async-start | bytes 8388608
Sparse Core Ops, SparseCore 0:
  12.3 48.8 all-gather.4
  63.5 45.3 all-gather.6
  111.9 46.6 reduce-scatter.2
  161.4 47.0 reduce-scatter.4

commit v4 on v3

--- a/solution.py
+++ b/solution.py
@@ -1,7 +1,7 @@
 import jax
 import jax.numpy as jnp
 from jax import lax
-from jax.sharding import PartitionSpec as P
+from jax.sharding import Mesh, PartitionSpec as P
 
 
 def silu_slope(value):
@@ -39,6 +39,44 @@
     return (out_part, in_part, gate_term, up_term, down_term)
 
 
+def y_shift(value, distance):
+    size = lax.axis_size("y")
+    return lax.ppermute(value, "y", [(i, (i + distance) % size) for i in range(size)])
+
+
+def core_swap(value):
+    return lax.ppermute(value, "core", [(0, 1), (1, 0)])
+
+
+def gather_rows(block):
+    cut = block.shape[0] // 2 // 8 * 8 + 8
+    from_prev = y_shift(block, 1)
+    from_next = y_shift(block, -1)
+    far = jnp.concatenate([y_shift(from_prev[:cut], 1), y_shift(from_next[cut:], -1)], axis=0)
+    mine = jnp.concatenate([block, from_prev, from_next, far], axis=0)
+    return jnp.concatenate([mine, core_swap(mine)], axis=0)
+
+
+def scatter_rows(parts):
+    half = parts.shape[0] // 2
+    slots = half // 4
+    cut = slots // 2 // 8 * 8 + 8
+    acc = parts[:half].astype(jnp.float32) + core_swap(parts[half:]).astype(jnp.float32)
+    own, prev, nxt, far = (acc[k * slots:(k + 1) * slots] for k in range(4))
+    prev = prev + jnp.pad(
+        y_shift(far[:cut].astype(jnp.bfloat16), -1).astype(jnp.float32), ((0, slots - cut), (0, 0))
+    )
+    nxt = nxt + jnp.pad(
+        y_shift(far[cut:].astype(jnp.bfloat16), 1).astype(jnp.float32), ((cut, 0), (0, 0))
+    )
+    total = (
+        own
+        + y_shift(prev.astype(jnp.bfloat16), -1).astype(jnp.float32)
+        + y_shift(nxt.astype(jnp.bfloat16), 1).astype(jnp.float32)
+    )
+    return total.astype(jnp.bfloat16)
+
+
 def shards(tokens, cotangent, counts, w_gate, w_up, w_down):
     rows_in = tokens[0]
     cot_in = cotangent[0]
@@ -46,7 +84,7 @@
     up_w = w_up[0]
     down_w = w_down[0]
     expert_pos = lax.axis_index("expert")
-    batch_pos = lax.axis_index("dp")
+    batch_pos = lax.axis_index("y") * lax.axis_size("core") + lax.axis_index("core")
     expert_ids = jnp.arange(counts.shape[0], dtype=jnp.int32)
     batch_ids = jnp.arange(counts.shape[1], dtype=jnp.int32)
     own_counts = jnp.sum(jnp.where(expert_ids[:, None] == expert_pos, counts, 0), axis=0)
@@ -55,18 +93,13 @@
     valid = (jnp.arange(slots, dtype=jnp.int32) < own_total)[:, None]
     masked = jnp.where(valid, rows_in, jnp.zeros_like(rows_in))
     masked_cot = jnp.where(valid, cot_in, jnp.zeros_like(cot_in))
-    all_rows = lax.all_gather(masked, "dp", axis=0, tiled=True)
-    all_cot = lax.all_gather(masked_cot, "dp", axis=0, tiled=True)
+    all_rows = gather_rows(masked)
+    all_cot = gather_rows(masked_cot)
     out_part, in_part, gate_term, up_term, down_term = expert_work(
         all_rows, all_cot, gate_w, up_w, down_w
     )
-    groups = lax.axis_size("dp")
-    outputs = lax.psum_scatter(
-        out_part.reshape(groups, slots, -1), "dp", scatter_dimension=0, tiled=False
-    )
-    input_grads = lax.psum_scatter(
-        in_part.astype(jnp.bfloat16).reshape(groups, slots, -1), "dp", scatter_dimension=0, tiled=False
-    )
+    outputs = scatter_rows(out_part)
+    input_grads = scatter_rows(in_part.astype(jnp.bfloat16))
     gate_grad = gate_term.astype(jnp.bfloat16)
     up_grad = up_term.astype(jnp.bfloat16)
     down_grad = down_term.astype(jnp.bfloat16)
@@ -74,24 +107,14 @@
 
 
 def solution(mesh):
-    placed = (
-        P("expert", "dp", None),
-        P("expert", "dp", None),
-        P(),
-        P("expert", None, "dp"),
-        P("expert", None, "dp"),
-        P("expert", "dp", None),
-    )
+    chips = mesh.shape["dp"] // 2
+    split = Mesh(mesh.devices.reshape(mesh.shape["expert"], chips, 2), ("expert", "y", "core"))
+    rows = P("expert", ("y", "core"), None)
+    cols = P("expert", None, ("y", "core"))
     return jax.shard_map(
         shards,
-        mesh=mesh,
-        in_specs=placed,
-        out_specs=(
-            P("expert", "dp", None),
-            P("expert", "dp", None),
-            P("expert", None, "dp"),
-            P("expert", None, "dp"),
-            P("expert", "dp", None),
-        ),
+        mesh=split,
+        in_specs=(rows, rows, P(), cols, cols, rows),
+        out_specs=(rows, rows, cols, cols, rows),
         check_vma=False,
     )

time: 215 us -> 346 us (1.61); the launches traced: 215 us -> 339 us
  local copies, waits for them, and re-layouts: 29.7 us -> 141 us
  starting transfers between devices: 0.34 us -> 25.4 us
  between operations: 13.8 us -> 0.91 us
  other arithmetic: 4.97 us -> 17.3 us
  waiting for transfers between devices: 115 us -> 109 us
  matrix products: 51.3 us -> 46.2 us
    concatenate x0 -> x4, local copies, waits for them, and re-layouts: none -> 129 us  [the longest x2 79.5 us: gather_rows(): return jnp.concatenate([mine, core_swap(mine)], axis=0)]
    ppermute x0 -> x20, waiting for transfers between devices: none -> 109 us  [the longest x16 109 us: y_shift(): lax.ppermute(value, 'y', [(i, (i + distance) % size) for i in range(size)])]
    all_gather x2 -> x0, waiting for transfers between devices: 66.8 us -> none  [the longest x1 48.2 us: shards(): all_rows = lax.all_gather(masked, 'dp', axis=0, tiled=True)]
    reduce_scatter x2 -> x0, waiting for transfers between devices: 47.4 us -> none  [the longest x1 47.4 us: shards(): lax.psum_scatter(in_part.astype(jnp.bfloat16).reshape(groups, slots, -1),...]
    ppermute x0 -> x20, starting transfers between devices: none -> 25.4 us  [the longest x16 20.9 us: y_shift(): lax.ppermute(value, 'y', [(i, (i + distance) % size) for i in range(size)])]
    reshape x2 -> x0, local copies, waits for them, and re-layouts: 13.9 us -> none  [the longest x1 6.95 us: shards(): in_part.astype(jnp.bfloat16).reshape(groups, slots, -1)]
    another operation x0 -> x2, other arithmetic: none -> 10.4 us
    unnamed x16 -> x38, local copies, waits for them, and re-layouts: 15.9 us -> 6.48 us
  transfers between devices with their start and end apart: 4 -> 20, of which waited for: 3 -> 10; matrix products, arithmetic and copies ran while one was open for 37% -> 50% of each run, Pallas kernels for 0% -> 0%
where the time goes in v4:
time: 346 us; the launch traced here: 339 us
  local copies, waits for them, and re-layouts  141 us (41%)
  waiting for transfers between devices  109 us (32%)
  matrix products  46.2 us (13%)
  starting transfers between devices  25.4 us (7%)
  other arithmetic  17.3 us (5%)
    ppermute x16, waiting for transfers between devices, y_shift(): lax.ppermute(value, 'y', [(i, (i + distance) % size) for i in range(size)])  109 us
    concatenate x2, local copies, waits for them, and re-layouts, gather_rows(): return jnp.concatenate([mine, core_swap(mine)], axis=0)  79.5 us
    concatenate x2, local copies, waits for them, and re-layouts, gather_rows(): mine = jnp.concatenate([block, from_prev, from_next, far], axis=0)  49.3 us
    ppermute x16, starting transfers between devices, y_shift(): lax.ppermute(value, 'y', [(i, (i + distance) % size) for i in range(size)])  20.9 us
    dot_general x3, matrix products, contract_last(): lax.dot_general(left, right, (((1,), (1,)), ((), ())), preferred_element_...  20.3 us
    dot_general x3, matrix products, contract_first(): lax.dot_general(left, right, (((0,), (0,)), ((), ())), preferred_element_...  15.2 us
    another operation x2, other arithmetic  10.4 us
  transfers between devices with their start and end apart: 20, of which 10 were waited for; matrix products, arithmetic and copies ran while one was open for 50% of the time, Pallas kernels for 0%

profile of v4, /device:TPU:1, one launch (start us, length us, event | category | flops | bytes accessed | tf_op | source)
XLA Modules:
  0.0 339.2 jit_solution(14440533857918616188)
XLA Ops:
  0.7 0.8 select_reduce_fusion
  1.5 0.6 fusion.23
  2.1 0.6 iota_compare_fusion.1
  2.7 1.6 bitcast_select_fusion
  4.4 2.2 collective-permute-start
  6.6 1.5 collective-permute-start.1
  8.1 19.9 %collective-permute-done = bf16[60,7168]{1,0:T(8,128)(2,1)S(1)} collective-permute-done((bf16[60,7168]{1,0:T(8,128)(2,1)S(1)}, bf16[60,7168]{1,0:T(8,128)(2,1)S(1)}, u32[]{:S(2)}, u32[]{:S(2)}) %collective-permute-start) | collective-permute-done | bytes 860192 | tf_op jit(solution)/shard_map/ppermute | solution.py:44
  28.0 0.1 collective-permute-start.2
  28.1 0.0 copy-start.3
  28.1 0.9 copy-done.3
  29.1 2.7 collective-permute-start.3
  31.8 8.2 %collective-permute-done.3 = bf16[28,7168]{1,0:T(8,128)(2,1)} collective-permute-done((bf16[28,7168]{1,0:T(8,128)(2,1)S(1)}, bf16[28,7168]{1,0:T(8,128)(2,1)}, u32[]{:S(2)}, u32[]{:S(2)}) %collective-permute-start.3) | collective-permute-done | bytes 401440 | tf_op jit(solution)/shard_map/ppermute | solution.py:44
  40.0 24.0 %concatenate.14 = bf16[240,7168]{1,0:T(8,128)(2,1)} concatenate(bf16[60,7168]{1,0:T(8,128)(2,1)S(1)} %get-tuple-element.24, bf16[60,7168]{1,0:T(8,128)(2,1)S(1)} %collective-permute-done, bf16[60,7168]{1,0:T(8,128)(2,1)} %copy-done.3, bf16[32,7168]{1,0:T(8,128)(2,1)S(1)} %collective-permute-done.2, bf16[28,7168]{1,0:T(8,128)(2,1)} %collective-permute-done.3), dimensions={0} | concatenate | bytes 6881280 | tf_op jit(solution)/shard_map/concatenate | solution.py:56
  64.0 2.5 collective-permute-start.4
  66.5 0.8 collective-permute-start.10
  67.2 2.7 collective-permute-start.11
  70.0 20.7 %collective-permute-done.10 = bf16[60,7168]{1,0:T(8,128)(2,1)S(1)} collective-permute-done((bf16[60,7168]{1,0:T(8,128)(2,1)S(1)}, bf16[60,7168]{1,0:T(8,128)(2,1)S(1)}, u32[]{:S(2)}, u32[]{:S(2)}) %collective-permute-start.10) | collective-permute-done | bytes 860192 | tf_op jit(solution)/shard_map/ppermute | solution.py:44
  90.7 0.1 collective-permute-start.12
  90.8 0.8 copy-done.4
  91.7 0.9 copy-done.6
  92.6 1.9 collective-permute-start.13
  94.4 9.7 %collective-permute-done.13 = bf16[28,7168]{1,0:T(8,128)(2,1)} collective-permute-done((bf16[28,7168]{1,0:T(8,128)(2,1)S(1)}, bf16[28,7168]{1,0:T(8,128)(2,1)}, u32[]{:S(2)}, u32[]{:S(2)}) %collective-permute-start.13) | collective-permute-done | bytes 401440 | tf_op jit(solution)/shard_map/ppermute | solution.py:44
  104.2 25.4 %concatenate.16 = bf16[240,7168]{1,0:T(8,128)(2,1)} concatenate(bf16[60,7168]{1,0:T(8,128)(2,1)S(1)} %get-tuple-element.23, bf16[60,7168]{1,0:T(8,128)(2,1)} %copy-done.4, bf16[60,7168]{1,0:T(8,128)(2,1)} %copy-done.6, bf16[32,7168]{1,0:T(8,128)(2,1)} %collective-permute-done.12, bf16[28,7168]{1,0:T(8,128)(2,1)} %collective-permute-done.13), dimensions={0} | concatenate | bytes 6881280 | tf_op jit(solution)/shard_map/concatenate | solution.py:56
  129.5 1.4 collective-permute-start.14
  131.0 40.7 %concatenate.15 = bf16[480,7168]{1,0:T(8,128)(2,1)} concatenate(bf16[60,7168]{1,0:T(8,128)(2,1)S(1)} %get-tuple-element.24, bf16[60,7168]{1,0:T(8,128)(2,1)S(1)} %collective-permute-done, bf16[60,7168]{1,0:T(8,128)(2,1)} %copy-done.3, bf16[32,7168]{1,0:T(8,128)(2,1)S(1)} %collective-permute-done.2, bf16[28,7168]{1,0:T(8,128)(2,1)} %collective-permute-done.3, ...), dimensions={0} | concatenate | bytes 13762560 | tf_op jit(solution)/shard_map/concatenate | solution.py:57
  171.7 6.1 %fusion.11 = f32[480,256]{1,0:T(8,128)S(1)} fusion(bf16[480,7168]{1,0:T(8,128)(2,1)} %concatenate.15, bf16[1,7168,256]{2,1,0:T(8,128)(2,1)} %param.9), kind=kOutput, calls=%fused_computation.18 | convolution fusion | flops 1761607680 | bytes 11042816 | tf_op jit(solution)/shard_map/dot_general | solution.py:25
  177.8 0.9 copy-done.8
  178.7 2.7 multiply_convert_fusion.2
  181.4 2.0 convolution_convert_fusion
  183.4 0.0 copy-start.7
  183.4 2.9 copy-done
  186.3 2.0 slice.67
  188.3 0.0 collective-permute-start.5
  188.3 38.8 %concatenate.17 = bf16[480,7168]{1,0:T(8,128)(2,1)} concatenate(bf16[60,7168]{1,0:T(8,128)(2,1)S(1)} %get-tuple-element.23, bf16[60,7168]{1,0:T(8,128)(2,1)S(1)} %copy-done.5, bf16[60,7168]{1,0:T(8,128)(2,1)S(1)} %copy-done.7, bf16[32,7168]{1,0:T(8,128)(2,1)} %collective-permute-done.12, bf16[28,7168]{1,0:T(8,128)(2,1)} %collective-permute-done.13, ...), dimensions={0} | concatenate | bytes 13762560 | tf_op jit(solution)/shard_map/concatenate | solution.py:57
  227.2 6.4 %multiply_convert_fusion = (bf16[480,256]{1,0:T(8,128)(2,1)S(1)}, bf16[480,256]{1,0:T(8,128)(2,1)S(1)}) fusion(f32[480,256]{1,0:T(8,128)} %copy-done.12, f32[480,256]{1,0:T(8,128)} %get-tuple-element.10, bf16[480,7168]{1,0:T(8,128)(2,1)} %concatenate.17, bf16[1,256,7168]{2,1,0:T(8,128)(2,1)} %param.11), kind=kOutput, calls=%fused_computation.38 | convolution fusion | flops 1763205120 | bytes 12025856 | tf_op jit(solution)/shard_map/dot_general | solution.py:13
  233.6 6.9 %fusion.9 = f32[480,7168]{1,0:T(8,128)} fusion(bf16[480,256]{1,0:T(8,128)(2,1)S(1)} %get-tuple-element.22, bf16[1,7168,256]{2,1,0:T(8,128)(2,1)S(1)} %copy-done.11), kind=kOutput, calls=%fused_computation.16 | convolution fusion | flops 1761607680 | bytes 17678336 | tf_op jit(solution)/shard_map/dot_general | solution.py:13
  240.5 7.0 %add_convert_fusion = bf16[480,7168]{1,0:T(8,128)(2,1)S(1)} fusion(f32[480,7168]{1,0:T(8,128)} %fusion.9, bf16[480,256]{1,0:T(8,128)(2,1)S(1)} %get-tuple-element.21, bf16[1,7168,256]{2,1,0:T(8,128)(2,1)S(1)} %copy-done.9), kind=kOutput, calls=%fused_computation | convolution fusion | flops 1768488960 | bytes 24559616 | tf_op jit(solution)/shard_map/dot_general | solution.py:13
  247.5 2.1 slice.92
  249.6 0.5 collective-permute-start.15
  250.1 7.1 %fusion.2 = bf16[1,256,7168]{2,1,0:T(8,128)(2,1)} fusion(bf16[480,256]{1,0:T(8,128)(2,1)S(1)} %get-tuple-element.12, bf16[480,7168]{1,0:T(8,128)(2,1)} %concatenate.17), kind=kOutput, calls=%fused_computation.7 | convolution fusion | flops 1763442688 | bytes 10797056 | tf_op jit(solution)/shard_map/dot_general | solution.py:19
  257.2 4.0 %fusion.1 = bf16[1,7168,256]{2,1,0:T(8,128)(2,1)} fusion(bf16[480,7168]{1,0:T(8,128)(2,1)S(1)} %bitcast.50, bf16[480,256]{1,0:T(8,128)(2,1)S(1)} %get-tuple-element.21), kind=kOutput, calls=%fused_computation.6 | convolution fusion | flops 1763442688 | bytes 10797056 | tf_op jit(solution)/shard_map/dot_general | solution.py:19
  261.2 4.0 %fusion = bf16[1,7168,256]{2,1,0:T(8,128)(2,1)} fusion(bf16[480,7168]{1,0:T(8,128)(2,1)S(1)} %bitcast.50, bf16[480,256]{1,0:T(8,128)(2,1)S(1)} %get-tuple-element.22), kind=kOutput, calls=%fused_computation.5 | convolution fusion | flops 1763442688 | bytes 10797056 | tf_op jit(solution)/shard_map/dot_general | solution.py:19
  265.3 6.1 %fusion.24 = (bf16[240,7168]{1,0:T(8,128)(2,1)S(1)}, f32[240,7168]{1,0:T(8,128)}) fusion(bf16[240,7168]{1,0:T(8,128)(2,1)} %collective-permute-done.5, bf16[480,7168]{1,0:T(8,128)(2,1)S(1)} %bitcast.46), kind=kLoop, calls=%fused_computation.47 | loop fusion | flops 6881280 | bytes 17203200 | tf_op jit(solution)/shard_map/convert.11
  271.4 0.9 slice.88
  272.3 0.1 slice.86
  272.4 3.1 collective-permute-start.6
  275.6 4.2 %fusion.25 = (bf16[240,7168]{1,0:T(8,128)(2,1)S(1)}, f32[240,7168]{1,0:T(8,128)}) fusion(bf16[240,7168]{1,0:T(8,128)(2,1)S(1)} %collective-permute-done.15, bf16[480,7168]{1,0:T(8,128)(2,1)S(1)} %add_convert_fusion), kind=kLoop, calls=%fused_computation.48 | loop fusion | flops 6881280 | bytes 17203200 | tf_op jit(solution)/shard_map/convert.9
  279.8 0.1 slice.97
  279.9 0.1 slice.95
  280.0 2.7 collective-permute-start.16
  282.8 6.0 %collective-permute-done.8 = bf16[28,7168]{1,0:T(8,128)(2,1)S(1)} collective-permute-done((bf16[28,7168]{1,0:T(8,128)(2,1)}, bf16[28,7168]{1,0:T(8,128)(2,1)S(1)}, u32[]{:S(2)}, u32[]{:S(2)}) %collective-permute-start.8) | collective-permute-done | bytes 401440 | tf_op jit(solution)/shard_map/ppermute | solution.py:44
  288.8 0.4 fusion.18
  289.2 0.1 collective-permute-start.7
  289.3 1.4 collective-permute-start.9
  290.7 7.9 %collective-permute-done.18 = bf16[28,7168]{1,0:T(8,128)(2,1)S(1)} collective-permute-done((bf16[28,7168]{1,0:T(8,128)(2,1)S(1)}, bf16[28,7168]{1,0:T(8,128)(2,1)S(1)}, u32[]{:S(2)}, u32[]{:S(2)}) %collective-permute-start.18) | collective-permute-done | bytes 401440 | tf_op jit(solution)/shard_map/ppermute | solution.py:44
  298.6 0.4 fusion.14
  299.0 0.1 collective-permute-start.17
  299.2 1.4 collective-permute-start.19
  300.6 14.4 %collective-permute-done.7 = bf16[60,7168]{1,0:T(8,128)(2,1)S(1)} collective-permute-done((bf16[60,7168]{1,0:T(8,128)(2,1)S(1)}, bf16[60,7168]{1,0:T(8,128)(2,1)S(1)}, u32[]{:S(2)}, u32[]{:S(2)}) %collective-permute-start.7) | collective-permute-done | bytes 860192 | tf_op jit(solution)/shard_map/ppermute | solution.py:44
  315.0 3.3 collective-permute-done.9
  318.3 1.3 fusion.21
  319.6 15.1 %collective-permute-done.17 = bf16[60,7168]{1,0:T(8,128)(2,1)S(1)} collective-permute-done((bf16[60,7168]{1,0:T(8,128)(2,1)S(1)}, bf16[60,7168]{1,0:T(8,128)(2,1)S(1)}, u32[]{:S(2)}, u32[]{:S(2)}) %collective-permute-start.17) | collective-permute-done | bytes 860192 | tf_op jit(solution)/shard_map/ppermute | solution.py:44
  334.6 3.3 collective-permute-done.19
  338.0 1.2 fusion.22
  (51 shorter events, 0.2 us)
Async XLA Ops:
  4.4 23.6 %collective-permute-start = (bf16[60,7168]{1,0:T(8,128)(2,1)S(1)}, bf16[60,7168]{1,0:T(8,128)(2,1)S(1)}, u32[]{:S(2)}, u32[]{:S(2)}) collective-permute-start(bf16[60,7168]{1,0:T(8,128)(2,1)S(1)} %get-tuple-element.24), channel_id=1, source_target_pairs={{0,2},{2,4},{4,6},{6,0},{1,3},{3,5},{5,7},{7,1},{8,10},{10,12},{12... | collective-permute-start | bytes 2580488 | tf_op jit(solution)/shard_map/ppermute | solution.py:44
  6.6 21.5 %collective-permute-start.1 = (bf16[60,7168]{1,0:T(8,128)(2,1)S(1)}, bf16[60,7168]{1,0:T(8,128)(2,1)S(1)}, u32[]{:S(2)}, u32[]{:S(2)}) collective-permute-start(bf16[60,7168]{1,0:T(8,128)(2,1)S(1)} %get-tuple-element.24), channel_id=1, source_target_pairs={{0,6},{2,0},{4,2},{6,4},{1,7},{3,1},{5,3},{7,5},{8,14},{10,8},{12,... | collective-permute-start | bytes 2580488 | tf_op jit(solution)/shard_map/ppermute | solution.py:44
  28.0 12.0 %collective-permute-start.2 = (bf16[32,7168]{1,0:T(8,128)(2,1)S(1)}, bf16[32,7168]{1,0:T(8,128)(2,1)S(1)}, u32[]{:S(2)}, u32[]{:S(2)}) collective-permute-start(bf16[32,7168]{1,0:T(8,128)(2,1)S(1)} %slice.82), channel_id=1, source_target_pairs={{0,2},{2,4},{4,6},{6,0},{1,3},{3,5},{5,7},{7,1},{8,10},{10,12},{12... | collective-permute-start | bytes 1376264 | tf_op jit(solution)/shard_map/ppermute | solution.py:44
  28.1 0.9 copy-start.3
  29.1 11.0 %collective-permute-start.3 = (bf16[28,7168]{1,0:T(8,128)(2,1)S(1)}, bf16[28,7168]{1,0:T(8,128)(2,1)}, u32[]{:S(2)}, u32[]{:S(2)}) collective-permute-start(bf16[28,7168]{1,0:T(8,128)(2,1)S(1)} %slice.83), channel_id=1, source_target_pairs={{0,6},{2,0},{4,2},{6,4},{1,7},{3,1},{5,3},{7,5},{8,14},{10,8},{12,... | collective-permute-start | bytes 1204232 | tf_op jit(solution)/shard_map/ppermute | solution.py:44
  64.0 67.0 %collective-permute-start.4 = (bf16[240,7168]{1,0:T(8,128)(2,1)}, bf16[240,7168]{1,0:T(8,128)(2,1)}, u32[]{:S(2)}, u32[]{:S(2)}) collective-permute-start(bf16[240,7168]{1,0:T(8,128)(2,1)} %concatenate.14), channel_id=1, source_target_pairs={{0,1},{1,0},{2,3},{3,2},{4,5},{5,4},{6,7},{7,6},{8,9},{9,8},{10,11... | collective-permute-start | bytes 10321928 | tf_op jit(solution)/shard_map/ppermute | solution.py:48
  66.5 24.2 %collective-permute-start.10 = (bf16[60,7168]{1,0:T(8,128)(2,1)S(1)}, bf16[60,7168]{1,0:T(8,128)(2,1)S(1)}, u32[]{:S(2)}, u32[]{:S(2)}) collective-permute-start(bf16[60,7168]{1,0:T(8,128)(2,1)S(1)} %get-tuple-element.23), channel_id=1, source_target_pairs={{0,2},{2,4},{4,6},{6,0},{1,3},{3,5},{5,7},{7,1},{8,10},{10,12},{12... | collective-permute-start | bytes 2580488 | tf_op jit(solution)/shard_map/ppermute | solution.py:44
  67.2 23.6 %collective-permute-start.11 = (bf16[60,7168]{1,0:T(8,128)(2,1)S(1)}, bf16[60,7168]{1,0:T(8,128)(2,1)S(1)}, u32[]{:S(2)}, u32[]{:S(2)}) collective-permute-start(bf16[60,7168]{1,0:T(8,128)(2,1)S(1)} %get-tuple-element.23), channel_id=1, source_target_pairs={{0,6},{2,0},{4,2},{6,4},{1,7},{3,1},{5,3},{7,5},{8,14},{10,8},{12,... | collective-permute-start | bytes 2580488 | tf_op jit(solution)/shard_map/ppermute | solution.py:44
  90.7 0.9 copy-start.4
  90.7 13.4 %collective-permute-start.12 = (bf16[32,7168]{1,0:T(8,128)(2,1)S(1)}, bf16[32,7168]{1,0:T(8,128)(2,1)}, u32[]{:S(2)}, u32[]{:S(2)}) collective-permute-start(bf16[32,7168]{1,0:T(8,128)(2,1)S(1)} %slice.89), channel_id=1, source_target_pairs={{0,2},{2,4},{4,6},{6,0},{1,3},{3,5},{5,7},{7,1},{8,10},{10,12},{12... | collective-permute-start | bytes 1376264 | tf_op jit(solution)/shard_map/ppermute | solution.py:44
  91.6 0.9 copy-start.6
  92.6 11.6 %collective-permute-start.13 = (bf16[28,7168]{1,0:T(8,128)(2,1)S(1)}, bf16[28,7168]{1,0:T(8,128)(2,1)}, u32[]{:S(2)}, u32[]{:S(2)}) collective-permute-start(bf16[28,7168]{1,0:T(8,128)(2,1)S(1)} %slice.90), channel_id=1, source_target_pairs={{0,6},{2,0},{4,2},{6,4},{1,7},{3,1},{5,3},{7,5},{8,14},{10,8},{12,... | collective-permute-start | bytes 1204232 | tf_op jit(solution)/shard_map/ppermute | solution.py:44
  129.5 58.8 %collective-permute-start.14 = (bf16[240,7168]{1,0:T(8,128)(2,1)}, bf16[240,7168]{1,0:T(8,128)(2,1)}, u32[]{:S(2)}, u32[]{:S(2)}) collective-permute-start(bf16[240,7168]{1,0:T(8,128)(2,1)} %concatenate.16), channel_id=1, source_target_pairs={{0,1},{1,0},{2,3},{3,2},{4,5},{5,4},{6,7},{7,6},{8,9},{9,8},{10,11... | collective-permute-start | bytes 10321928 | tf_op jit(solution)/shard_map/ppermute | solution.py:48
  171.7 6.1 %copy-start.2 = (bf16[480,7168]{1,0:T(8,128)(2,1)S(1)}, bf16[480,7168]{1,0:T(8,128)(2,1)}, u32[]{:S(2)}) copy-start(bf16[480,7168]{1,0:T(8,128)(2,1)} %concatenate.15) | copy-start | bytes 20643844
  171.7 7.0 %copy-start.8 = (bf16[1,7168,256]{2,1,0:T(8,128)(2,1)S(1)}, bf16[1,7168,256]{2,1,0:T(8,128)(2,1)}, u32[]{:S(2)}) copy-start(bf16[1,7168,256]{2,1,0:T(8,128)(2,1)} %param.10) | copy-start | bytes 11010052
  178.7 2.7 copy-start.12
  178.7 2.7 copy-start.10
  183.4 3.0 copy-start
  183.4 4.9 %copy-start.5 = (bf16[60,7168]{1,0:T(8,128)(2,1)S(1)}, bf16[60,7168]{1,0:T(8,128)(2,1)}, u32[]{:S(2)}) copy-start(bf16[60,7168]{1,0:T(8,128)(2,1)} %copy-done.4) | copy-start | bytes 2580484
  183.4 4.9 %copy-start.7 = (bf16[60,7168]{1,0:T(8,128)(2,1)S(1)}, bf16[60,7168]{1,0:T(8,128)(2,1)}, u32[]{:S(2)}) copy-start(bf16[60,7168]{1,0:T(8,128)(2,1)} %copy-done.6) | copy-start | bytes 2580484
  188.3 77.0 %collective-permute-start.5 = (bf16[240,7168]{1,0:T(8,128)(2,1)}, bf16[240,7168]{1,0:T(8,128)(2,1)}, u32[]{:S(2)}, u32[]{:S(2)}) collective-permute-start(bf16[240,7168]{1,0:T(8,128)(2,1)} %slice.67), channel_id=1, source_target_pairs={{0,1},{1,0},{2,3},{3,2},{4,5},{5,4},{6,7},{7,6},{8,9},{9,8},{10,11... | collective-permute-start | bytes 10321928 | tf_op jit(solution)/shard_map/ppermute | solution.py:48
  227.2 6.4 %copy-start.11 = (bf16[1,7168,256]{2,1,0:T(8,128)(2,1)S(1)}, bf16[1,7168,256]{2,1,0:T(8,128)(2,1)}, u32[]{:S(2)}) copy-start(bf16[1,7168,256]{2,1,0:T(8,128)(2,1)} %param.9) | copy-start | bytes 11010052
  233.6 6.9 %copy-start.9 = (bf16[1,7168,256]{2,1,0:T(8,128)(2,1)S(1)}, bf16[1,7168,256]{2,1,0:T(8,128)(2,1)}, u32[]{:S(2)}) copy-start(bf16[1,7168,256]{2,1,0:T(8,128)(2,1)} %param.10) | copy-start | bytes 11010052
  247.5 9.7 %slice-start.4 = ((s8[6881280]{0:T(1024)(128)(4,1)}), s8[2686976]{0:T(1024)(128)(4,1)S(1)}, s32[]{:S(2)}) async-start(s8[6881280]{0:T(1024)(128)(4,1)} %bitcast.49), calls=%async_computation.4 | async-start | bytes 5373952
  249.6 7.6 %slice-start.5 = ((s8[6881280]{0:T(1024)(128)(4,1)}), s8[4194304]{0:T(1024)(128)(4,1)S(1)}, s32[]{:S(2)}) async-start(s8[6881280]{0:T(1024)(128)(4,1)} %bitcast.49), calls=%async_computation.5 | async-start | bytes 8388608
  249.6 26.0 %collective-permute-start.15 = (bf16[240,7168]{1,0:T(8,128)(2,1)}, bf16[240,7168]{1,0:T(8,128)(2,1)S(1)}, u32[]{:S(2)}, u32[]{:S(2)}) collective-permute-start(bf16[240,7168]{1,0:T(8,128)(2,1)} %slice.92), channel_id=1, source_target_pairs={{0,1},{1,0},{2,3},{3,2},{4,5},{5,4},{6,7},{7,6},{8,9},{9,8},{10,11... | collective-permute-start | bytes 10321928 | tf_op jit(solution)/shard_map/ppermute | solution.py:48
  257.2 8.1 %slice-start = ((s8[6881280]{0:T(1024)(128)(4,1)}), s8[4194304]{0:T(1024)(128)(4,1)S(1)}, s32[]{:S(2)}) async-start(s8[6881280]{0:T(1024)(128)(4,1)} %bitcast.45), calls=%async_computation | async-start | bytes 8388608
  261.2 4.1 %slice-start.1 = ((s8[6881280]{0:T(1024)(128)(4,1)}), s8[2686976]{0:T(1024)(128)(4,1)S(1)}, s32[]{:S(2)}) async-start(s8[6881280]{0:T(1024)(128)(4,1)} %bitcast.45), calls=%async_computation.1 | async-start | bytes 5373952
  272.3 16.5 %slice-start.2 = ((s8[6881280]{0:T(1024)(128)(4,1)}), s8[4194304]{0:T(1024)(128)(4,1)S(1)}, s32[]{:S(2)}) async-start(s8[6881280]{0:T(1024)(128)(4,1)} %bitcast.47), calls=%async_computation.2 | async-start | bytes 8388608
  272.4 16.4 %slice-start.3 = ((s8[6881280]{0:T(1024)(128)(4,1)}), s8[2686976]{0:T(1024)(128)(4,1)S(1)}, s32[]{:S(2)}) async-start(s8[6881280]{0:T(1024)(128)(4,1)} %bitcast.47), calls=%async_computation.3 | async-start | bytes 5373952
  272.4 16.4 %collective-permute-start.6 = (bf16[32,7168]{1,0:T(8,128)(2,1)S(1)}, bf16[32,7168]{1,0:T(8,128)(2,1)S(1)}, u32[]{:S(2)}, u32[]{:S(2)}) collective-permute-start(bf16[32,7168]{1,0:T(8,128)(2,1)S(1)} %slice.86), channel_id=1, source_target_pairs={{0,6},{2,0},{4,2},{6,4},{1,7},{3,1},{5,3},{7,5},{8,14},{10,8},{12,... | collective-permute-start | bytes 1376264 | tf_op jit(solution)/shard_map/ppermute | solution.py:44
  275.6 13.2 %collective-permute-start.8 = (bf16[28,7168]{1,0:T(8,128)(2,1)}, bf16[28,7168]{1,0:T(8,128)(2,1)S(1)}, u32[]{:S(2)}, u32[]{:S(2)}) collective-permute-start(bf16[28,7168]{1,0:T(8,128)(2,1)} %slice.88), channel_id=1, source_target_pairs={{0,2},{2,4},{4,6},{6,0},{1,3},{3,5},{5,7},{7,1},{8,10},{10,12},{12... | collective-permute-start | bytes 1204232 | tf_op jit(solution)/shard_map/ppermute | solution.py:44
  279.9 18.7 %copy-start.1 = (f32[240,7168]{1,0:T(8,128)S(1)}, f32[240,7168]{1,0:T(8,128)}, u32[]{:S(2)}) copy-start(f32[240,7168]{1,0:T(8,128)} %get-tuple-element.14) | copy-start | bytes 20643844
  280.0 18.6 %collective-permute-start.16 = (bf16[32,7168]{1,0:T(8,128)(2,1)S(1)}, bf16[32,7168]{1,0:T(8,128)(2,1)S(1)}, u32[]{:S(2)}, u32[]{:S(2)}) collective-permute-start(bf16[32,7168]{1,0:T(8,128)(2,1)S(1)} %slice.95), channel_id=1, source_target_pairs={{0,6},{2,0},{4,2},{6,4},{1,7},{3,1},{5,3},{7,5},{8,14},{10,8},{12,... | collective-permute-start | bytes 1376264 | tf_op jit(solution)/shard_map/ppermute | solution.py:44
  282.8 15.8 %collective-permute-start.18 = (bf16[28,7168]{1,0:T(8,128)(2,1)S(1)}, bf16[28,7168]{1,0:T(8,128)(2,1)S(1)}, u32[]{:S(2)}, u32[]{:S(2)}) collective-permute-start(bf16[28,7168]{1,0:T(8,128)(2,1)S(1)} %slice.97), channel_id=1, source_target_pairs={{0,2},{2,4},{4,6},{6,0},{1,3},{3,5},{5,7},{7,1},{8,10},{10,12},{12... | collective-permute-start | bytes 1204232 | tf_op jit(solution)/shard_map/ppermute | solution.py:44
  289.2 25.8 %collective-permute-start.7 = (bf16[60,7168]{1,0:T(8,128)(2,1)S(1)}, bf16[60,7168]{1,0:T(8,128)(2,1)S(1)}, u32[]{:S(2)}, u32[]{:S(2)}) collective-permute-start(bf16[60,7168]{1,0:T(8,128)(2,1)S(1)} %get-tuple-element.19), channel_id=1, source_target_pairs={{0,6},{2,0},{4,2},{6,4},{1,7},{3,1},{5,3},{7,5},{8,14},{10,8},{12,... | collective-permute-start | bytes 2580488 | tf_op jit(solution)/shard_map/ppermute | solution.py:44
  289.3 29.0 %collective-permute-start.9 = (bf16[60,7168]{1,0:T(8,128)(2,1)S(1)}, bf16[60,7168]{1,0:T(8,128)(2,1)S(1)}, u32[]{:S(2)}, u32[]{:S(2)}) collective-permute-start(bf16[60,7168]{1,0:T(8,128)(2,1)S(1)} %get-tuple-element.20), channel_id=1, source_target_pairs={{0,2},{2,4},{4,6},{6,0},{1,3},{3,5},{5,7},{7,1},{8,10},{10,12},{12... | collective-permute-start | bytes 2580488 | tf_op jit(solution)/shard_map/ppermute | solution.py:44
  299.0 35.6 %collective-permute-start.17 = (bf16[60,7168]{1,0:T(8,128)(2,1)S(1)}, bf16[60,7168]{1,0:T(8,128)(2,1)S(1)}, u32[]{:S(2)}, u32[]{:S(2)}) collective-permute-start(bf16[60,7168]{1,0:T(8,128)(2,1)S(1)} %get-tuple-element.17), channel_id=1, source_target_pairs={{0,6},{2,0},{4,2},{6,4},{1,7},{3,1},{5,3},{7,5},{8,14},{10,8},{12,... | collective-permute-start | bytes 2580488 | tf_op jit(solution)/shard_map/ppermute | solution.py:44
  299.2 38.8 %collective-permute-start.19 = (bf16[60,7168]{1,0:T(8,128)(2,1)S(1)}, bf16[60,7168]{1,0:T(8,128)(2,1)S(1)}, u32[]{:S(2)}, u32[]{:S(2)}) collective-permute-start(bf16[60,7168]{1,0:T(8,128)(2,1)S(1)} %get-tuple-element.18), channel_id=1, source_target_pairs={{0,2},{2,4},{4,6},{6,0},{1,3},{3,5},{5,7},{7,1},{8,10},{10,12},{12... | collective-permute-start | bytes 2580488 | tf_op jit(solution)/shard_map/ppermute | solution.py:44
